TPU v7x, 256 devices: a whole 4x4x8 slice. The times are simulated.
256 devices in a mesh: subj: 16 (over x, y), gz: 4 (over z_hi, core), gy: 4 (over z_lo).
Axes of the slice: x: 4, y: 4, z: 8 (z_hi: 2, z_lo: 4; z = z_hi * 4 + z_lo), core: 2. Of those that a mesh axis runs over, the one named last changes fastest.
Arguments:
- subjects: float32 [16, 32, 32, 640], P('subj', 'gz', 'gy'), may hold values from -6 to 6
- templates: float32 [4, 32, 32, 640], P(None, 'gz', 'gy'), may hold values from -6 to 6
- group_of: int32 [16], replicated, may hold values from 0 to 3, as said below
- extents: int32 [16, 4], replicated, may hold values from 0 to 32, as said below
Outputs:
- new_templates: float32 [4, 32, 32, 640], P(None, 'gz', 'gy')
- velocity: float32 [3, 32, 32, 640], P(None, 'gz', 'gy')
Inputs may be any that keep to these rules, and one draw needn't show every extreme that they name: `extents`: columns are z_lo, z_hi, y_lo, y_hi of one subject in whole-volume indices, with 1 <= z_lo < z_hi <= 32 and 0 <= y_lo < y_hi <= 32. `group_of`: subjects 0 and 1 are in different groups.
All inputs are finite; a program needn't handle non-finite values.
Results may differ from a plain program's by a relative error of at most 0.00002.
Values sent between devices are 32-bit elements; how exact they have to be, the bound alone decides.
No kernel may reach another device: no remote copies, remote signals or barrier semaphores. Data moves between devices by JAX's collectives and lax.ppermute only.
A program may use at most 64 MiB of HBM per device.

v0:
```python
from functools import partial
from functools import reduce

import jax
import jax.numpy as jnp
from jax import lax
from jax.sharding import PartitionSpec as P

BOX_EPS = 1e-05
SPREAD = (0.0625, 0.25, 0.375, 0.25, 0.0625)


def padded_2(x, sides, width):
    for axis, dim in sides:
        peers, length = (lax.axis_size(axis), x.shape[dim])
        up = [(i, (i + 1) % peers) for i in range(peers - 1)]
        down = [(j, i) for i, j in up]
        last = lax.slice_in_dim(x, length - width, length, axis=dim)
        initial = lax.slice_in_dim(x, 0, width, axis=dim)
        before = lax.ppermute(last, axis, up)
        after = lax.ppermute(initial, axis, down)
        x = jnp.concatenate([before, x, after], axis=dim)
    return x


def add_pair(former, latter):
    return former + latter


def window_sum(volume, along_axis, length, extent):
    pieces = [
        lax.slice_in_dim(volume, offset, offset + length, axis=along_axis)
        for offset in range(extent)
    ]
    return reduce(add_pair, pieces)


def weighted(volume, along_axis, length):
    pieces = [
        SPREAD[offset] * lax.slice_in_dim(volume, offset, offset + length, axis=along_axis)
        for offset in range(5)
    ]
    return reduce(add_pair, pieces)


def box_local(padded, slab_depth, slab_rows):
    widened = jnp.pad(padded, ((0, 0), (0, 0), (4, 4)))
    along_x = window_sum(widened, 2, padded.shape[2], 9)
    along_y = window_sum(along_x, 1, slab_rows, 9)
    return window_sum(along_y, 0, slab_depth, 9)


def smooth_local(padded, slab_depth, slab_rows):
    widened = jnp.pad(padded, ((0, 0), (0, 0), (2, 2)))
    along_x = weighted(widened, 2, padded.shape[2])
    along_y = weighted(along_x, 1, slab_rows)
    return weighted(along_y, 0, slab_depth)


def template_stats(templ_pad, slab_depth, slab_rows):
    templ_mean = box_local(templ_pad, slab_depth, slab_rows) / 729.0
    templ_var = (
        box_local(templ_pad * templ_pad, slab_depth, slab_rows) / 729.0
        - templ_mean * templ_mean
        + BOX_EPS
    )
    return (templ_mean, templ_var)


def region_masks(extents, z_index, y_index):
    inside_z = (z_index[None, :] >= extents[:, 0:1]) & (z_index[None, :] < extents[:, 1:2])
    inside_y = (y_index[None, :] >= extents[:, 2:3]) & (y_index[None, :] < extents[:, 3:4])
    return (inside_z[:, :, None] & inside_y[:, None, :]).astype(jnp.float32)


def subject_force(image_pad, templ_pad, templ_mean, templ_var, region_mask, slab_depth, slab_rows):
    mean_i = box_local(image_pad, slab_depth, slab_rows) / 729.0
    square_mean = box_local(image_pad * image_pad, slab_depth, slab_rows) / 729.0
    cross_mean = box_local(image_pad * templ_pad, slab_depth, slab_rows) / 729.0
    var_i = square_mean - mean_i * mean_i + BOX_EPS
    covariance = cross_mean - mean_i * templ_mean
    image_mid = image_pad[4 : 4 + slab_depth, 4 : 4 + slab_rows, :]
    templ_mid = templ_pad[4 : 4 + slab_depth, 4 : 4 + slab_rows, :]
    centred_i = image_mid - mean_i
    centred_t = templ_mid - templ_mean
    factor = (
        region_mask
        * (2.0 * covariance / (var_i * templ_var))
        * (centred_t - covariance / var_i * centred_i)
    )
    grad_z = 0.5 * (
        image_pad[5 : 5 + slab_depth, 4 : 4 + slab_rows, :]
        - image_pad[3 : 3 + slab_depth, 4 : 4 + slab_rows, :]
    )
    grad_y = 0.5 * (
        image_pad[4 : 4 + slab_depth, 5 : 5 + slab_rows, :]
        - image_pad[4 : 4 + slab_depth, 3 : 3 + slab_rows, :]
    )
    side_pad = jnp.pad(image_mid, ((0, 0), (0, 0), (1, 1)))
    grad_x = 0.5 * (side_pad[:, :, 2:] - side_pad[:, :, :-2])
    force_field = jnp.stack([factor * grad_z, factor * grad_y, factor * grad_x])
    return (force_field, region_mask * image_mid)


def local(subjects, templates, group_of, extents):
    local_subjects, slab_depth, slab_rows, cell_count = subjects.shape
    groups = templates.shape[0]
    smoother = jax.vmap(partial(smooth_local, slab_depth=slab_depth, slab_rows=slab_rows))
    volumes = jnp.concatenate([templates, subjects], axis=0)
    padded = padded_2(volumes, (("gz", 1), ("gy", 2)), 4)
    templ_all = padded[:groups]
    image_all = padded[groups:]
    templ_mean, templ_var = jax.vmap(
        partial(template_stats, slab_depth=slab_depth, slab_rows=slab_rows)
    )(templ_all)
    z_index = lax.axis_index("gz") * slab_depth + jnp.arange(slab_depth, dtype=jnp.int32)
    y_index = lax.axis_index("gy") * slab_rows + jnp.arange(slab_rows, dtype=jnp.int32)
    all_masks = region_masks(extents, z_index, y_index)
    onehot = (group_of[:, None] == jnp.arange(groups, dtype=jnp.int32)[None, :]).astype(jnp.float32)
    counts = jnp.sum(onehot[:, :, None, None] * all_masks[:, None], axis=0)
    denominator = jnp.maximum(counts, 1.0)[..., None]
    first_subject = lax.axis_index("subj") * local_subjects

    def advance(totals, subject_index):
        global_index = first_subject + subject_index
        group_index = group_of[global_index]
        region_mask = all_masks[global_index][:, :, None]
        force_field, masked = subject_force(
            image_all[subject_index],
            templ_all[group_index],
            templ_mean[group_index],
            templ_var[group_index],
            region_mask,
            slab_depth,
            slab_rows,
        )
        return ((totals[0].at[group_index].add(masked), totals[1] + force_field), None)

    start = (
        jnp.zeros(templates.shape, jnp.float32),
        jnp.zeros((3, slab_depth, slab_rows, cell_count), jnp.float32),
    )
    totals, unused = lax.scan(advance, start, jnp.arange(local_subjects, dtype=jnp.int32))
    template_sum, velocity_sum = lax.psum((totals[0], totals[1]), "subj")
    new_templates = template_sum / denominator
    summed_pad = padded_2(velocity_sum, (("gz", 1), ("gy", 2)), 2)
    velocity = smoother(summed_pad)
    return (new_templates, velocity)


def solution(mesh):
    in_specs = (P("subj", "gz", "gy", None), P(None, "gz", "gy", None), P(), P())
    out_specs = (P(None, "gz", "gy", None), P(None, "gz", "gy", None))
    return jax.shard_map(local, mesh=mesh, in_specs=in_specs, out_specs=out_specs, check_vma=False)
```

profile of v0, /device:TPU:1, one launch (start us, length us, event | category | flops | bytes accessed | tf_op | source)
XLA Modules:
  0.0 245.2 jit_solution(12785508724708914255)
XLA Ops:
  9.5 10.2 %collective-permute-start = (f32[5,4,8,640]{3,1,2,0:T(4,128)S(1)}, f32[5,4,8,640]{3,1,2,0:T(4,128)S(1)}, u32[]{:S(2)}, u32[]{:S(2)}) collective-permute-start(f32[5,4,8,640]{3,1,2,0:T(4,128)S(1)} %get-tuple-element.70), channel_id=1, source_target_pairs={{0,4},{4,8},{8,12},{1,5},{5,9},{9,13},{2,6},{6,10},{10,14},{3,7},{... | collective-permute-start | bytes 1228808 | tf_op jit(solution)/shard_map/ppermute | solution.py:20
  19.7 1.9 collective-permute-start.1
  21.7 2.9 %collective-permute-done = f32[5,4,8,640]{3,1,2,0:T(4,128)S(1)} collective-permute-done((f32[5,4,8,640]{3,1,2,0:T(4,128)S(1)}, f32[5,4,8,640]{3,1,2,0:T(4,128)S(1)}, u32[]{:S(2)}, u32[]{:S(2)}) %collective-permute-start) | collective-permute-done | bytes 409632 | tf_op jit(solution)/shard_map/ppermute | solution.py:20
  24.6 16.1 %collective-permute-done.1 = f32[5,4,8,640]{3,1,2,0:T(4,128)S(1)} collective-permute-done((f32[5,4,8,640]{3,1,2,0:T(4,128)S(1)}, f32[5,4,8,640]{3,1,2,0:T(4,128)S(1)}, u32[]{:S(2)}, u32[]{:S(2)}) %collective-permute-start.1) | collective-permute-done | bytes 409632 | tf_op jit(solution)/shard_map/ppermute | solution.py:21
  41.0 1.3 fusion.86
  42.3 2.7 %collective-permute-start.2 = (f32[5,16,4,640]{3,1,2,0:T(8,128)}, f32[5,16,4,640]{3,1,2,0:T(8,128)S(1)}, u32[]{:S(2)}, u32[]{:S(2)}) collective-permute-start(f32[5,16,4,640]{3,1,2,0:T(8,128)} %get-tuple-element.62), channel_id=1, source_target_pairs={{0,1},{1,2},{2,3},{4,5},{5,6},{6,7},{8,9},{9,10},{10,11},{12,13},{... | collective-permute-start | bytes 2457608 | tf_op jit(solution)/shard_map/ppermute | solution.py:20
  45.0 1.3 collective-permute-start.3
  49.8 4.7 %collective-permute-done.2 = f32[5,16,4,640]{3,1,2,0:T(8,128)S(1)} collective-permute-done((f32[5,16,4,640]{3,1,2,0:T(8,128)}, f32[5,16,4,640]{3,1,2,0:T(8,128)S(1)}, u32[]{:S(2)}, u32[]{:S(2)}) %collective-permute-start.2) | collective-permute-done | bytes 819232 | tf_op jit(solution)/shard_map/ppermute | solution.py:20
  54.5 4.0 %collective-permute-done.3 = f32[5,16,4,640]{3,1,2,0:T(8,128)S(1)} collective-permute-done((f32[5,16,4,640]{3,1,2,0:T(8,128)}, f32[5,16,4,640]{3,1,2,0:T(8,128)S(1)}, u32[]{:S(2)}, u32[]{:S(2)}) %collective-permute-start.3) | collective-permute-done | bytes 819232 | tf_op jit(solution)/shard_map/ppermute | solution.py:21
  58.5 1.9 fusion.85
  62.2 2.8 %fusion.43 = (f32[16,16,640]{2,0,1:T(8,128)S(1)}, f32[16,16,640]{2,0,1:T(8,128)S(1)}, f32[16,16,640]{2,0,1:T(8,128)S(1)}) fusion(f32[16,16,640]{2,0,1:T(8,128)S(1)} %get-tuple-element.59, f32[16,16,640]{2,0,1:T(8,128)S(1)} %get-tuple-element.57), kind=kLoop, calls=%fused_computation.114 | loop fusion | flops 2785280 | bytes 3276800 | tf_op jit(solution)/shard_map/while/body/eval_jaxpr/add | solution.py:27
  65.0 1.4 fusion.51
  67.4 29.5 %fusion.7 = (f32[4,16,16,640]{3,1,2,0:T(8,128)S(1)}, f32[4,16,16,640]{3,1,2,0:T(8,128)}) fusion(f32[4,16,16,640]{3,1,2,0:T(8,128)} %copy-done, f32[4,16,16,640]{3,1,2,0:T(8,128)} %get-tuple-element.60), kind=kLoop, calls=%fused_computation.23 | loop fusion | flops 10485760 | bytes 10485760 | tf_op jit(solution)/shard_map/vmap()/add | solution.py:27
  97.0 6.2 %slice_add_fusion = f32[4,16,8,640]{3,1,2,0:T(8,128)S(1)} fusion(f32[4,16,16,640]{3,1,2,0:T(8,128)} %get-tuple-element.84), kind=kLoop, calls=%fused_computation.50 | loop fusion | flops 2621440 | bytes 13107200 | tf_op jit(solution)/shard_map/vmap()/add | solution.py:27
  105.2 1.5 fusion.66
  108.8 92.8 %all-reduce.10.cloned.1.call-done = (f32[4,8,8,640]{3,2,1,0:T(8,128)}, f32[3,8,8,640]{3,1,2,0:T(8,128)}) async-done(((f32[4,8,8,640]{3,2,1,0:T(8,128)}, f32[3,8,8,640]{3,1,2,0:T(8,128)}), (f32[4,8,8,640]{3,2,1,0:T(8,128)}, f32[3,8,8,640]{3,1,2,0:T(8,128)})) %all-reduce.10.cloned.1.call-update) | async-done | bytes 1146896 | tf_op jit(solution)/shard_map/psum | solution.py:144
  201.6 1.4 fusion.88
  203.0 9.5 %collective-permute-start.4 = (f32[3,2,8,640]{3,1,2,0:T(2,128)S(1)}, f32[3,2,8,640]{3,1,2,0:T(2,128)S(1)}, u32[]{:S(2)}, u32[]{:S(2)}) collective-permute-start(f32[3,2,8,640]{3,1,2,0:T(2,128)S(1)} %get-tuple-element.77), channel_id=1, source_target_pairs={{0,4},{4,8},{8,12},{1,5},{5,9},{9,13},{2,6},{6,10},{10,14},{3,7},{... | collective-permute-start | bytes 368648 | tf_op jit(solution)/shard_map/ppermute | solution.py:20
  212.4 1.9 collective-permute-start.5
  214.4 9.3 %collective-permute-done.5 = f32[3,2,8,640]{3,1,2,0:T(2,128)S(1)} collective-permute-done((f32[3,2,8,640]{3,1,2,0:T(2,128)S(1)}, f32[3,2,8,640]{3,1,2,0:T(2,128)S(1)}, u32[]{:S(2)}, u32[]{:S(2)}) %collective-permute-start.5) | collective-permute-done | bytes 122912 | tf_op jit(solution)/shard_map/ppermute | solution.py:21
  224.7 3.5 %collective-permute-start.6 = (f32[3,12,2,640]{3,1,2,0:T(8,128)S(1)}, f32[3,12,2,640]{3,1,2,0:T(8,128)S(1)}, u32[]{:S(2)}, u32[]{:S(2)}) collective-permute-start(f32[3,12,2,640]{3,1,2,0:T(8,128)S(1)} %get-tuple-element.72), channel_id=1, source_target_pairs={{0,1},{1,2},{2,3},{4,5},{5,6},{6,7},{8,9},{9,10},{10,11},{12,13},{... | collective-permute-start | bytes 552968 | tf_op jit(solution)/shard_map/ppermute | solution.py:20
  228.3 1.3 collective-permute-start.7
  231.4 3.8 %collective-permute-done.7 = f32[3,12,2,640]{3,1,2,0:T(8,128)S(1)} collective-permute-done((f32[3,12,2,640]{3,1,2,0:T(8,128)S(1)}, f32[3,12,2,640]{3,1,2,0:T(8,128)S(1)}, u32[]{:S(2)}, u32[]{:S(2)}) %collective-permute-start.7) | collective-permute-done | bytes 184352 | tf_op jit(solution)/shard_map/ppermute | solution.py:21
  235.4 1.6 fusion.20
  (59 shorter events, 15.4 us)
Async XLA Ops:
  7.2 14.5 %copy-start.7 = (s32[16,4]{0,1:T(4,128)S(1)}, s32[16,4]{0,1:T(4,128)}, u32[]{:S(2)}) copy-start(s32[16,4]{0,1:T(4,128)} %param.9) | copy-start | bytes 772
  7.2 194.4 %all-reduce.10.cloned.1.call-start = ((), (), s32[]{:S(2)}) async-start(), calls=%async_computation | async-start | bytes 2293760 | tf_op jit(solution)/shard_map/psum | solution.py:144
  9.5 15.1 %collective-permute-start = (f32[5,4,8,640]{3,1,2,0:T(4,128)S(1)}, f32[5,4,8,640]{3,1,2,0:T(4,128)S(1)}, u32[]{:S(2)}, u32[]{:S(2)}) collective-permute-start(f32[5,4,8,640]{3,1,2,0:T(4,128)S(1)} %get-tuple-element.70), channel_id=1, source_target_pairs={{0,4},{4,8},{8,12},{1,5},{5,9},{9,13},{2,6},{6,10},{10,14},{3,7},{... | collective-permute-start | bytes 1228808 | tf_op jit(solution)/shard_map/ppermute | solution.py:20
  19.7 20.9 %collective-permute-start.1 = (f32[5,4,8,640]{3,1,2,0:T(4,128)S(1)}, f32[5,4,8,640]{3,1,2,0:T(4,128)S(1)}, u32[]{:S(2)}, u32[]{:S(2)}) collective-permute-start(f32[5,4,8,640]{3,1,2,0:T(4,128)S(1)} %get-tuple-element.71), channel_id=1, source_target_pairs={{4,0},{8,4},{12,8},{5,1},{9,5},{13,9},{6,2},{10,6},{14,10},{7,3},{... | collective-permute-start | bytes 1228808 | tf_op jit(solution)/shard_map/ppermute | solution.py:21
  40.9 5.4 %copy-start.8 = (s32[16]{0:T(128)S(1)}, s32[16]{0:T(128)}, u32[]{:S(2)}) copy-start(s32[16]{0:T(128)} %param.8) | copy-start | bytes 196
  40.9 8.2 %copy-start.9 = (s32[4]{0:T(128)S(1)}, s32[4]{0:T(128)}, u32[]{:S(2)}) copy-start(s32[4]{0:T(128)} %constant.82.clone.1) | copy-start | bytes 52
  42.3 12.2 %collective-permute-start.2 = (f32[5,16,4,640]{3,1,2,0:T(8,128)}, f32[5,16,4,640]{3,1,2,0:T(8,128)S(1)}, u32[]{:S(2)}, u32[]{:S(2)}) collective-permute-start(f32[5,16,4,640]{3,1,2,0:T(8,128)} %get-tuple-element.62), channel_id=1, source_target_pairs={{0,1},{1,2},{2,3},{4,5},{5,6},{6,7},{8,9},{9,10},{10,11},{12,13},{... | collective-permute-start | bytes 2457608 | tf_op jit(solution)/shard_map/ppermute | solution.py:20
  45.0 13.5 %collective-permute-start.3 = (f32[5,16,4,640]{3,1,2,0:T(8,128)}, f32[5,16,4,640]{3,1,2,0:T(8,128)S(1)}, u32[]{:S(2)}, u32[]{:S(2)}) collective-permute-start(f32[5,16,4,640]{3,1,2,0:T(8,128)} %get-tuple-element.63), channel_id=1, source_target_pairs={{1,0},{2,1},{3,2},{5,4},{6,5},{7,6},{9,8},{10,9},{11,10},{13,12},{... | collective-permute-start | bytes 2457608 | tf_op jit(solution)/shard_map/ppermute | solution.py:21
  60.4 1.8 copy-start
  62.2 2.8 %copy-start.2 = (f32[16,16,640]{2,0,1:T(8,128)}, f32[16,16,640]{2,0,1:T(8,128)S(1)}, u32[]{:S(2)}) copy-start(f32[16,16,640]{2,0,1:T(8,128)S(1)} %get-tuple-element.59) | copy-start | bytes 1966084
  104.0 1.0 copy-start.1
  104.0 1.2 copy-start.3
  107.6 1.0 copy-start.5
  201.6 28.0 %copy-start.6 = (f32[4,8,8,640]{3,2,1,0:T(8,128)S(1)}, f32[4,8,8,640]{3,2,1,0:T(8,128)}, u32[]{:S(2)}) copy-start(f32[4,8,8,640]{3,2,1,0:T(8,128)} %get-tuple-element.53) | copy-start | bytes 1966084
  201.6 33.6 %copy-start.4 = (f32[3,8,8,640]{3,1,2,0:T(8,128)S(1)}, f32[3,8,8,640]{3,1,2,0:T(8,128)}, u32[]{:S(2)}) copy-start(f32[3,8,8,640]{3,1,2,0:T(8,128)} %get-tuple-element.54) | copy-start | bytes 1474564
  203.0 11.4 %collective-permute-start.4 = (f32[3,2,8,640]{3,1,2,0:T(2,128)S(1)}, f32[3,2,8,640]{3,1,2,0:T(2,128)S(1)}, u32[]{:S(2)}, u32[]{:S(2)}) collective-permute-start(f32[3,2,8,640]{3,1,2,0:T(2,128)S(1)} %get-tuple-element.77), channel_id=1, source_target_pairs={{0,4},{4,8},{8,12},{1,5},{5,9},{9,13},{2,6},{6,10},{10,14},{3,7},{... | collective-permute-start | bytes 368648 | tf_op jit(solution)/shard_map/ppermute | solution.py:20
  212.4 11.2 %collective-permute-start.5 = (f32[3,2,8,640]{3,1,2,0:T(2,128)S(1)}, f32[3,2,8,640]{3,1,2,0:T(2,128)S(1)}, u32[]{:S(2)}, u32[]{:S(2)}) collective-permute-start(f32[3,2,8,640]{3,1,2,0:T(2,128)S(1)} %get-tuple-element.78), channel_id=1, source_target_pairs={{4,0},{8,4},{12,8},{5,1},{9,5},{13,9},{6,2},{10,6},{14,10},{7,3},{... | collective-permute-start | bytes 368648 | tf_op jit(solution)/shard_map/ppermute | solution.py:21
  224.7 6.6 %collective-permute-start.6 = (f32[3,12,2,640]{3,1,2,0:T(8,128)S(1)}, f32[3,12,2,640]{3,1,2,0:T(8,128)S(1)}, u32[]{:S(2)}, u32[]{:S(2)}) collective-permute-start(f32[3,12,2,640]{3,1,2,0:T(8,128)S(1)} %get-tuple-element.72), channel_id=1, source_target_pairs={{0,1},{1,2},{2,3},{4,5},{5,6},{6,7},{8,9},{9,10},{10,11},{12,13},{... | collective-permute-start | bytes 552968 | tf_op jit(solution)/shard_map/ppermute | solution.py:20
  228.3 6.9 %collective-permute-start.7 = (f32[3,12,2,640]{3,1,2,0:T(8,128)S(1)}, f32[3,12,2,640]{3,1,2,0:T(8,128)S(1)}, u32[]{:S(2)}, u32[]{:S(2)}) collective-permute-start(f32[3,12,2,640]{3,1,2,0:T(8,128)S(1)} %get-tuple-element.73), channel_id=1, source_target_pairs={{1,0},{2,1},{3,2},{5,4},{6,5},{7,6},{9,8},{10,9},{11,10},{13,12},{... | collective-permute-start | bytes 552968 | tf_op jit(solution)/shard_map/ppermute | solution.py:21
Sparse Core Ops, SparseCore 0:
  108.7 92.8 all-reduce.9
where the time goes:
time: 246 us; the launch traced here: 245 us
  waiting for transfers between devices  134 us (54%)
  other arithmetic  54 us (22%)
  starting transfers between devices  32.4 us (13%)
  between operations  16.3 us (7%)
  local copies, waits for them, and re-layouts  8.18 us (3%)
    psum x1, waiting for transfers between devices, local(): template_sum, velocity_sum = lax.psum((totals[0], totals[1]), 'subj')  92.8 us
    add x12, other arithmetic, add_pair(): return former + latter  43.8 us
    ppermute x4, waiting for transfers between devices, padded_2(): after = lax.ppermute(initial, axis, down)  33.1 us
    ppermute x4, starting transfers between devices, padded_2(): before = lax.ppermute(last, axis, up)  25.9 us
    ppermute x4, waiting for transfers between devices, padded_2(): before = lax.ppermute(last, axis, up)  8.46 us
    ppermute x4, starting transfers between devices, padded_2(): after = lax.ppermute(initial, axis, down)  6.43 us
  transfers between devices with their start and end apart: 9, of which 8 were waited for; matrix products, arithmetic and copies ran while one was open for 1% of the time, Pallas kernels for 0%

commit v1 on v0

--- a/solution.py
+++ b/solution.py
@@ -73,7 +73,8 @@
     return (inside_z[:, :, None] & inside_y[:, None, :]).astype(jnp.float32)
 
 
-def subject_force(image_pad, templ_pad, templ_mean, templ_var, region_mask, slab_depth, slab_rows):
+def subject_force(image_pad, templ_pad, region_mask, slab_depth, slab_rows):
+    templ_mean, templ_var = template_stats(templ_pad, slab_depth, slab_rows)
     mean_i = box_local(image_pad, slab_depth, slab_rows) / 729.0
     square_mean = box_local(image_pad * image_pad, slab_depth, slab_rows) / 729.0
     cross_mean = box_local(image_pad * templ_pad, slab_depth, slab_rows) / 729.0
@@ -98,51 +99,64 @@
     )
     side_pad = jnp.pad(image_mid, ((0, 0), (0, 0), (1, 1)))
     grad_x = 0.5 * (side_pad[:, :, 2:] - side_pad[:, :, :-2])
-    force_field = jnp.stack([factor * grad_z, factor * grad_y, factor * grad_x])
-    return (force_field, region_mask * image_mid)
+    return jnp.stack([factor * grad_z, factor * grad_y, factor * grad_x])
+
+
+def scatter_sum(pieces, axis):
+    received = lax.all_to_all(pieces, axis, 0, 0, tiled=True)
+    return received
+
+
+def gather_all(part, axis):
+    peers = lax.axis_size(axis)
+    copies = jnp.broadcast_to(part[None], (peers,) + part.shape)
+    return lax.all_to_all(copies, axis, 0, 0, tiled=True)
 
 
 def local(subjects, templates, group_of, extents):
     local_subjects, slab_depth, slab_rows, cell_count = subjects.shape
     groups = templates.shape[0]
+    peers = lax.axis_size("subj")
+    cells = slab_depth * slab_rows * cell_count
+    chunk = cells // peers
     smoother = jax.vmap(partial(smooth_local, slab_depth=slab_depth, slab_rows=slab_rows))
-    volumes = jnp.concatenate([templates, subjects], axis=0)
-    padded = padded_2(volumes, (("gz", 1), ("gy", 2)), 4)
-    templ_all = padded[:groups]
-    image_all = padded[groups:]
-    templ_mean, templ_var = jax.vmap(
-        partial(template_stats, slab_depth=slab_depth, slab_rows=slab_rows)
-    )(templ_all)
+    first_subject = lax.axis_index("subj") * local_subjects
+    own_groups = lax.dynamic_slice_in_dim(group_of, first_subject, local_subjects)
+    own_templates = jnp.take(templates, own_groups, axis=0)
     z_index = lax.axis_index("gz") * slab_depth + jnp.arange(slab_depth, dtype=jnp.int32)
     y_index = lax.axis_index("gy") * slab_rows + jnp.arange(slab_rows, dtype=jnp.int32)
     all_masks = region_masks(extents, z_index, y_index)
+    own_masks = lax.dynamic_slice_in_dim(all_masks, first_subject, local_subjects)
     onehot = (group_of[:, None] == jnp.arange(groups, dtype=jnp.int32)[None, :]).astype(jnp.float32)
     counts = jnp.sum(onehot[:, :, None, None] * all_masks[:, None], axis=0)
     denominator = jnp.maximum(counts, 1.0)[..., None]
-    first_subject = lax.axis_index("subj") * local_subjects
 
-    def advance(totals, subject_index):
-        global_index = first_subject + subject_index
-        group_index = group_of[global_index]
-        region_mask = all_masks[global_index][:, :, None]
-        force_field, masked = subject_force(
-            image_all[subject_index],
-            templ_all[group_index],
-            templ_mean[group_index],
-            templ_var[group_index],
-            region_mask,
-            slab_depth,
-            slab_rows,
-        )
-        return ((totals[0].at[group_index].add(masked), totals[1] + force_field), None)
+    masked = own_masks[..., None] * subjects
+    pieces = masked.reshape(local_subjects, peers, chunk).transpose(1, 0, 2)
+    arrived = scatter_sum(pieces, "subj").reshape(peers * local_subjects, chunk)
+    group_parts = jnp.stack(
+        [
+            jnp.sum(jnp.where((group_of == g)[:, None], arrived, 0.0), axis=0)
+            for g in range(groups)
+        ]
+    )
+    group_full = gather_all(group_parts, "subj")
+    template_sum = group_full.transpose(1, 0, 2).reshape(templates.shape)
+    new_templates = template_sum / denominator
 
-    start = (
-        jnp.zeros(templates.shape, jnp.float32),
-        jnp.zeros((3, slab_depth, slab_rows, cell_count), jnp.float32),
-    )
-    totals, unused = lax.scan(advance, start, jnp.arange(local_subjects, dtype=jnp.int32))
-    template_sum, velocity_sum = lax.psum((totals[0], totals[1]), "subj")
-    new_templates = template_sum / denominator
+    volumes = jnp.concatenate([own_templates, subjects], axis=0)
+    padded = padded_2(volumes, (("gz", 1), ("gy", 2)), 4)
+    templ_all = padded[:local_subjects]
+    image_all = padded[local_subjects:]
+    forces = jax.vmap(
+        partial(subject_force, slab_depth=slab_depth, slab_rows=slab_rows)
+    )(image_all, templ_all, own_masks[..., None])
+    force_sum = jnp.sum(forces, axis=0)
+
+    force_pieces = force_sum.reshape(3, peers, chunk).transpose(1, 0, 2)
+    force_part = jnp.sum(scatter_sum(force_pieces, "subj"), axis=0)
+    force_full = gather_all(force_part, "subj")
+    velocity_sum = force_full.transpose(1, 0, 2).reshape(3, slab_depth, slab_rows, cell_count)
     summed_pad = padded_2(velocity_sum, (("gz", 1), ("gy", 2)), 2)
     velocity = smoother(summed_pad)
     return (new_templates, velocity)

time: 246 us -> 138 us (0.56)
  waiting for transfers between devices: 134 us -> 56.8 us
  other arithmetic: 54 us -> 14.8 us
  starting transfers between devices: 32.4 us -> 54.2 us
  between operations: 16.3 us -> 3.1 us
    psum x1 -> x0, waiting for transfers between devices: 92.8 us -> none  [local(): template_sum, velocity_sum = lax.psum((totals[0], totals[1]), 'subj')]
    add x12 -> x13, other arithmetic: 43.8 us -> 10.4 us  [add_pair(): return former + latter]
    all_to_all x0 -> x4, waiting for transfers between devices: none -> 24.7 us  [the longest x2 15.4 us: scatter_sum(): received = lax.all_to_all(pieces, axis, 0, 0, tiled=True)]
    all_to_all x0 -> x4, starting transfers between devices: none -> 17.5 us  [the longest x2 10.3 us: scatter_sum(): received = lax.all_to_all(pieces, axis, 0, 0, tiled=True)]
    ppermute x4, waiting for transfers between devices: 33.1 us -> 28.3 us  [padded_2(): after = lax.ppermute(initial, axis, down)]
    ppermute x4, waiting for transfers between devices: 8.46 us -> 3.82 us  [padded_2(): before = lax.ppermute(last, axis, up)]
    ppermute x4, starting transfers between devices: 25.9 us -> 30.3 us  [padded_2(): before = lax.ppermute(last, axis, up)]
    another operation x5 -> x1, other arithmetic: 3.86 us -> 0.05 us  [local(): jnp.stack([jnp.sum(jnp.where((group_of == g)[:, None], arrived, 0.0), axi...]
  transfers between devices with their start and end apart: 9 -> 12, of which waited for: 8 -> 10; matrix products, arithmetic and copies ran while one was open for 1% -> 2% of each run, Pallas kernels for 0% -> 0%
where the time goes in v1:
time: 138 us; the launch traced here: 137 us
  waiting for transfers between devices  56.8 us (41%)
  starting transfers between devices  54.2 us (39%)
  other arithmetic  14.8 us (11%)
  local copies, waits for them, and re-layouts  8.4 us (6%)
  between operations  3.1 us (2%)
    ppermute x4, starting transfers between devices, padded_2(): before = lax.ppermute(last, axis, up)  30.3 us
    ppermute x4, waiting for transfers between devices, padded_2(): after = lax.ppermute(initial, axis, down)  28.3 us
    all_to_all x2, waiting for transfers between devices, scatter_sum(): received = lax.all_to_all(pieces, axis, 0, 0, tiled=True)  15.4 us
    add x13, other arithmetic, add_pair(): return former + latter  10.4 us
    all_to_all x2, starting transfers between devices, scatter_sum(): received = lax.all_to_all(pieces, axis, 0, 0, tiled=True)  10.3 us
    all_to_all x2, waiting for transfers between devices, gather_all(): return lax.all_to_all(copies, axis, 0, 0, tiled=True)  9.31 us
    all_to_all x2, starting transfers between devices, gather_all(): return lax.all_to_all(copies, axis, 0, 0, tiled=True)  7.19 us
    ppermute x4, starting transfers between devices, padded_2(): after = lax.ppermute(initial, axis, down)  6.43 us
  transfers between devices with their start and end apart: 12, of which 10 were waited for; matrix products, arithmetic and copies ran while one was open for 2% of the time, Pallas kernels for 0%

profile of v1, /device:TPU:1, one launch (start us, length us, event | category | flops | bytes accessed | tf_op | source)
XLA Modules:
  0.0 137.4 jit_solution(6346898137892720625)
XLA Ops:
  6.1 10.2 %collective-permute-start = (f32[2,4,8,640]{3,1,2,0:T(4,128)S(1)}, f32[2,4,8,640]{3,1,2,0:T(4,128)S(1)}, u32[]{:S(2)}, u32[]{:S(2)}) collective-permute-start(f32[2,4,8,640]{3,1,2,0:T(4,128)S(1)} %get-tuple-element.35), channel_id=1, source_target_pairs={{0,4},{4,8},{8,12},{1,5},{5,9},{9,13},{2,6},{6,10},{10,14},{3,7},{... | collective-permute-start | bytes 491528 | tf_op jit(solution)/shard_map/ppermute | solution.py:20
  16.3 1.9 %collective-permute-start.1 = (f32[2,4,8,640]{3,1,2,0:T(4,128)S(1)}, f32[2,4,8,640]{3,1,2,0:T(4,128)S(1)}, u32[]{:S(2)}, u32[]{:S(2)}) collective-permute-start(f32[2,4,8,640]{3,1,2,0:T(4,128)S(1)} %get-tuple-element.34), channel_id=1, source_target_pairs={{4,0},{8,4},{12,8},{5,1},{9,5},{13,9},{6,2},{10,6},{14,10},{7,3},{... | collective-permute-start | bytes 491528 | tf_op jit(solution)/shard_map/ppermute | solution.py:21
  18.6 10.1 %collective-permute-done.1 = f32[2,4,8,640]{3,1,2,0:T(4,128)S(1)} collective-permute-done((f32[2,4,8,640]{3,1,2,0:T(4,128)S(1)}, f32[2,4,8,640]{3,1,2,0:T(4,128)S(1)}, u32[]{:S(2)}, u32[]{:S(2)}) %collective-permute-start.1) | collective-permute-done | bytes 163872 | tf_op jit(solution)/shard_map/ppermute | solution.py:21
  28.8 3.8 %collective-permute-start.2 = (f32[2,16,4,640]{3,1,2,0:T(8,128)S(1)}, f32[2,16,4,640]{3,1,2,0:T(8,128)S(1)}, u32[]{:S(2)}, u32[]{:S(2)}) collective-permute-start(f32[2,16,4,640]{3,1,2,0:T(8,128)S(1)} %get-tuple-element.28), channel_id=1, source_target_pairs={{0,1},{1,2},{2,3},{4,5},{5,6},{6,7},{8,9},{9,10},{10,11},{12,13},{... | collective-permute-start | bytes 983048 | tf_op jit(solution)/shard_map/ppermute | solution.py:20
  33.9 2.7 %collective-permute-done.2 = f32[2,16,4,640]{3,1,2,0:T(8,128)S(1)} collective-permute-done((f32[2,16,4,640]{3,1,2,0:T(8,128)S(1)}, f32[2,16,4,640]{3,1,2,0:T(8,128)S(1)}, u32[]{:S(2)}, u32[]{:S(2)}) %collective-permute-start.2) | collective-permute-done | bytes 327712 | tf_op jit(solution)/shard_map/ppermute | solution.py:20
  36.6 3.8 %collective-permute-done.3 = f32[2,16,4,640]{3,1,2,0:T(8,128)S(1)} collective-permute-done((f32[2,16,4,640]{3,1,2,0:T(8,128)S(1)}, f32[2,16,4,640]{3,1,2,0:T(8,128)S(1)}, u32[]{:S(2)}, u32[]{:S(2)}) %collective-permute-start.3) | collective-permute-done | bytes 327712 | tf_op jit(solution)/shard_map/ppermute | solution.py:21
  40.8 1.4 %fusion.51 = f32[1,16,16,640]{3,1,2,0:T(8,128)S(1)} fusion(f32[1,16,16,640]{3,1,2,0:T(8,128)S(1)} %get-tuple-element.23), kind=kLoop, calls=%fused_computation.102 | loop fusion | flops 1310720 | bytes 1310720 | tf_op jit(solution)/shard_map/vmap()/add | solution.py:27
  42.3 1.4 %fusion.35 = f32[1,16,16,640]{3,1,2,0:T(8,128)S(1)} fusion(f32[1,16,16,640]{3,1,2,0:T(8,128)S(1)} %get-tuple-element.24), kind=kLoop, calls=%fused_computation.86 | loop fusion | flops 1310720 | bytes 1310720 | tf_op jit(solution)/shard_map/vmap()/add | solution.py:27
  43.8 1.4 %fusion.27 = f32[1,16,16,640]{3,1,2,0:T(8,128)S(1)} fusion(f32[1,16,16,640]{3,1,2,0:T(8,128)S(1)} %get-tuple-element.25), kind=kLoop, calls=%fused_computation.78 | loop fusion | flops 1310720 | bytes 1310720 | tf_op jit(solution)/shard_map/vmap()/add | solution.py:27
  45.3 1.4 %fusion.19 = f32[1,16,16,640]{3,1,2,0:T(8,128)S(1)} fusion(f32[1,16,16,640]{3,1,2,0:T(8,128)S(1)} %get-tuple-element.21), kind=kLoop, calls=%fused_computation.70 | loop fusion | flops 1310720 | bytes 1310720 | tf_op jit(solution)/shard_map/vmap()/add | solution.py:27
  46.8 1.4 %fusion.43 = f32[1,16,16,640]{3,1,2,0:T(8,128)S(1)} fusion(f32[1,16,16,640]{3,1,2,0:T(8,128)S(1)} %get-tuple-element.22), kind=kLoop, calls=%fused_computation.94 | loop fusion | flops 1310720 | bytes 1310720 | tf_op jit(solution)/shard_map/vmap()/add | solution.py:27
  51.6 6.8 %all-to-all-start.2 = ((f32[16,3,2560]{2,1,0:T(4,128)}), f32[16,3,2560]{2,1,0:T(4,128)S(1)}, u32[]{:S(2)}, u32[]{:S(2)}) async-start(f32[16,3,2560]{2,1,0:T(4,128)} %copy.43), calls=%async_computation.2 | async-start | bytes 1310720 | tf_op jit(solution)/shard_map/all_to_all | solution.py:106
  59.2 8.8 %all-to-all-done.2 = f32[16,3,2560]{2,1,0:T(4,128)S(1)} async-done(((f32[16,3,2560]{2,1,0:T(4,128)}), f32[16,3,2560]{2,1,0:T(4,128)S(1)}, u32[]{:S(2)}, u32[]{:S(2)}) %all-to-all-start.2) | async-done | bytes 491552 | tf_op jit(solution)/shard_map/all_to_all | solution.py:106
  68.0 3.5 %all-to-all-start = ((f32[16,1,2560]{2,1,0:T(1,128)}), f32[16,1,2560]{2,1,0:T(1,128)S(1)}, u32[]{:S(2)}, u32[]{:S(2)}) async-start(f32[16,1,2560]{2,1,0:T(1,128)} %transpose_reshape.3), calls=%async_computation | async-start | bytes 327680 | tf_op jit(solution)/shard_map/all_to_all | solution.py:106
  71.7 6.6 %all-to-all-done = f32[16,1,2560]{2,1,0:T(1,128)S(1)} async-done(((f32[16,1,2560]{2,1,0:T(1,128)}), f32[16,1,2560]{2,1,0:T(1,128)S(1)}, u32[]{:S(2)}, u32[]{:S(2)}) %all-to-all-start) | async-done | bytes 163872 | tf_op jit(solution)/shard_map/all_to_all | solution.py:106
  79.2 3.6 %all-to-all-start.3 = ((f32[16,3,2560]{2,1,0:T(4,128)}), f32[16,3,2560]{2,1,0:T(4,128)S(1)}, u32[]{:S(2)}, u32[]{:S(2)}) async-start(f32[16,3,2560]{2,1,0:T(4,128)} %broadcast_in_dim.80), calls=%async_computation.3 | async-start | bytes 1310720 | tf_op jit(solution)/shard_map/all_to_all | solution.py:113
  83.1 9.3 %all-to-all-done.3 = f32[16,3,2560]{2,1,0:T(4,128)S(1)} async-done(((f32[16,3,2560]{2,1,0:T(4,128)}), f32[16,3,2560]{2,1,0:T(4,128)S(1)}, u32[]{:S(2)}, u32[]{:S(2)}) %all-to-all-start.3) | async-done | bytes 491552 | tf_op jit(solution)/shard_map/all_to_all | solution.py:113
  93.3 3.6 %all-to-all-start.1 = ((f32[16,4,2560]{2,1,0:T(4,128)}), f32[16,4,2560]{2,1,0:T(4,128)S(1)}, u32[]{:S(2)}, u32[]{:S(2)}) async-start(f32[16,4,2560]{2,1,0:T(4,128)} %broadcast_in_dim.76), calls=%async_computation.1 | async-start | bytes 1310720 | tf_op jit(solution)/shard_map/all_to_all | solution.py:113
  97.5 10.0 %collective-permute-start.4 = (f32[3,2,8,640]{3,2,1,0:T(8,128)S(1)}, f32[3,2,8,640]{3,2,1,0:T(8,128)S(1)}, u32[]{:S(2)}, u32[]{:S(2)}) collective-permute-start(f32[3,2,8,640]{3,2,1,0:T(8,128)S(1)} %get-tuple-element.31), channel_id=1, source_target_pairs={{0,4},{4,8},{8,12},{1,5},{5,9},{9,13},{2,6},{6,10},{10,14},{3,7},{... | collective-permute-start | bytes 368648 | tf_op jit(solution)/shard_map/ppermute | solution.py:20
  107.9 1.9 %collective-permute-start.5 = (f32[3,2,8,640]{3,2,1,0:T(8,128)S(1)}, f32[3,2,8,640]{3,2,1,0:T(8,128)S(1)}, u32[]{:S(2)}, u32[]{:S(2)}) collective-permute-start(f32[3,2,8,640]{3,2,1,0:T(8,128)S(1)} %get-tuple-element.30), channel_id=1, source_target_pairs={{4,0},{8,4},{12,8},{5,1},{9,5},{13,9},{6,2},{10,6},{14,10},{7,3},{... | collective-permute-start | bytes 368648 | tf_op jit(solution)/shard_map/ppermute | solution.py:21
  109.9 10.6 %collective-permute-done.5 = f32[3,2,8,640]{3,2,1,0:T(8,128)S(1)} collective-permute-done((f32[3,2,8,640]{3,2,1,0:T(8,128)S(1)}, f32[3,2,8,640]{3,2,1,0:T(8,128)S(1)}, u32[]{:S(2)}, u32[]{:S(2)}) %collective-permute-start.5) | collective-permute-done | bytes 122912 | tf_op jit(solution)/shard_map/ppermute | solution.py:21
  120.7 6.4 %collective-permute-start.6 = (f32[3,12,2,640]{3,1,2,0:T(8,128)S(1)}, f32[3,12,2,640]{3,1,2,0:T(8,128)S(1)}, u32[]{:S(2)}, u32[]{:S(2)}) collective-permute-start(f32[3,12,2,640]{3,1,2,0:T(8,128)S(1)} %copy.45), channel_id=1, source_target_pairs={{0,1},{1,2},{2,3},{4,5},{5,6},{6,7},{8,9},{9,10},{10,11},{12,13},{... | collective-permute-start | bytes 552968 | tf_op jit(solution)/shard_map/ppermute | solution.py:20
  130.3 3.8 %collective-permute-done.7 = f32[3,12,2,640]{3,1,2,0:T(8,128)S(1)} collective-permute-done((f32[3,12,2,640]{3,1,2,0:T(8,128)S(1)}, f32[3,12,2,640]{3,1,2,0:T(8,128)S(1)}, u32[]{:S(2)}, u32[]{:S(2)}) %collective-permute-start.7) | collective-permute-done | bytes 184352 | tf_op jit(solution)/shard_map/ppermute | solution.py:21
  134.4 1.6 %fusion.4 = f32[3,12,12,640]{3,2,1,0:T(8,128)S(1)} fusion(f32[3,12,12,640]{3,2,1,0:T(8,128)S(1)} %pad_maximum_fusion), kind=kLoop, calls=%fused_computation.8 | loop fusion | flops 2488320 | bytes 2211840 | tf_op jit(solution)/shard_map/vmap()/add | solution.py:27
  (76 shorter events, 18.3 us)
Async XLA Ops:
  0.6 4.4 %copy-start = (f32[4,8,8,640]{3,2,1,0:T(8,128)S(1)}, f32[4,8,8,640]{3,2,1,0:T(8,128)}, u32[]{:S(2)}) copy-start(f32[4,8,8,640]{3,2,1,0:T(8,128)} %param.5) | copy-start | bytes 1966084
  6.1 12.4 %collective-permute-start = (f32[2,4,8,640]{3,1,2,0:T(4,128)S(1)}, f32[2,4,8,640]{3,1,2,0:T(4,128)S(1)}, u32[]{:S(2)}, u32[]{:S(2)}) collective-permute-start(f32[2,4,8,640]{3,1,2,0:T(4,128)S(1)} %get-tuple-element.35), channel_id=1, source_target_pairs={{0,4},{4,8},{8,12},{1,5},{5,9},{9,13},{2,6},{6,10},{10,14},{3,7},{... | collective-permute-start | bytes 491528 | tf_op jit(solution)/shard_map/ppermute | solution.py:20
  16.3 12.3 %collective-permute-start.1 = (f32[2,4,8,640]{3,1,2,0:T(4,128)S(1)}, f32[2,4,8,640]{3,1,2,0:T(4,128)S(1)}, u32[]{:S(2)}, u32[]{:S(2)}) collective-permute-start(f32[2,4,8,640]{3,1,2,0:T(4,128)S(1)} %get-tuple-element.34), channel_id=1, source_target_pairs={{4,0},{8,4},{12,8},{5,1},{9,5},{13,9},{6,2},{10,6},{14,10},{7,3},{... | collective-permute-start | bytes 491528 | tf_op jit(solution)/shard_map/ppermute | solution.py:21
  28.8 7.7 %collective-permute-start.2 = (f32[2,16,4,640]{3,1,2,0:T(8,128)S(1)}, f32[2,16,4,640]{3,1,2,0:T(8,128)S(1)}, u32[]{:S(2)}, u32[]{:S(2)}) collective-permute-start(f32[2,16,4,640]{3,1,2,0:T(8,128)S(1)} %get-tuple-element.28), channel_id=1, source_target_pairs={{0,1},{1,2},{2,3},{4,5},{5,6},{6,7},{8,9},{9,10},{10,11},{12,13},{... | collective-permute-start | bytes 983048 | tf_op jit(solution)/shard_map/ppermute | solution.py:20
  32.6 7.8 %collective-permute-start.3 = (f32[2,16,4,640]{3,1,2,0:T(8,128)S(1)}, f32[2,16,4,640]{3,1,2,0:T(8,128)S(1)}, u32[]{:S(2)}, u32[]{:S(2)}) collective-permute-start(f32[2,16,4,640]{3,1,2,0:T(8,128)S(1)} %get-tuple-element.29), channel_id=1, source_target_pairs={{1,0},{2,1},{3,2},{5,4},{6,5},{7,6},{9,8},{10,9},{11,10},{13,12},{... | collective-permute-start | bytes 983048 | tf_op jit(solution)/shard_map/ppermute | solution.py:21
  48.2 0.9 copy-start.1
  50.4 21.1 %copy-start.2 = (s32[16]{0:T(128)S(1)}, s32[16]{0:T(128)}, u32[]{:S(2)}) copy-start(s32[16]{0:T(128)} %param.6) | copy-start | bytes 196
  51.6 16.4 %all-to-all-start.2 = ((f32[16,3,2560]{2,1,0:T(4,128)}), f32[16,3,2560]{2,1,0:T(4,128)S(1)}, u32[]{:S(2)}, u32[]{:S(2)}) async-start(f32[16,3,2560]{2,1,0:T(4,128)} %copy.43), calls=%async_computation.2 | async-start | bytes 1310720 | tf_op jit(solution)/shard_map/all_to_all | solution.py:106
  68.0 10.3 %all-to-all-start = ((f32[16,1,2560]{2,1,0:T(1,128)}), f32[16,1,2560]{2,1,0:T(1,128)S(1)}, u32[]{:S(2)}, u32[]{:S(2)}) async-start(f32[16,1,2560]{2,1,0:T(1,128)} %transpose_reshape.3), calls=%async_computation | async-start | bytes 327680 | tf_op jit(solution)/shard_map/all_to_all | solution.py:106
  79.2 13.2 %all-to-all-start.3 = ((f32[16,3,2560]{2,1,0:T(4,128)}), f32[16,3,2560]{2,1,0:T(4,128)S(1)}, u32[]{:S(2)}, u32[]{:S(2)}) async-start(f32[16,3,2560]{2,1,0:T(4,128)} %broadcast_in_dim.80), calls=%async_computation.3 | async-start | bytes 1310720 | tf_op jit(solution)/shard_map/all_to_all | solution.py:113
  93.3 14.1 %all-to-all-start.1 = ((f32[16,4,2560]{2,1,0:T(4,128)}), f32[16,4,2560]{2,1,0:T(4,128)S(1)}, u32[]{:S(2)}, u32[]{:S(2)}) async-start(f32[16,4,2560]{2,1,0:T(4,128)} %broadcast_in_dim.76), calls=%async_computation.1 | async-start | bytes 1310720 | tf_op jit(solution)/shard_map/all_to_all | solution.py:113
  97.5 12.3 %collective-permute-start.4 = (f32[3,2,8,640]{3,2,1,0:T(8,128)S(1)}, f32[3,2,8,640]{3,2,1,0:T(8,128)S(1)}, u32[]{:S(2)}, u32[]{:S(2)}) collective-permute-start(f32[3,2,8,640]{3,2,1,0:T(8,128)S(1)} %get-tuple-element.31), channel_id=1, source_target_pairs={{0,4},{4,8},{8,12},{1,5},{5,9},{9,13},{2,6},{6,10},{10,14},{3,7},{... | collective-permute-start | bytes 368648 | tf_op jit(solution)/shard_map/ppermute | solution.py:20
  107.9 12.6 %collective-permute-start.5 = (f32[3,2,8,640]{3,2,1,0:T(8,128)S(1)}, f32[3,2,8,640]{3,2,1,0:T(8,128)S(1)}, u32[]{:S(2)}, u32[]{:S(2)}) collective-permute-start(f32[3,2,8,640]{3,2,1,0:T(8,128)S(1)} %get-tuple-element.30), channel_id=1, source_target_pairs={{4,0},{8,4},{12,8},{5,1},{9,5},{13,9},{6,2},{10,6},{14,10},{7,3},{... | collective-permute-start | bytes 368648 | tf_op jit(solution)/shard_map/ppermute | solution.py:21
  120.7 9.5 %collective-permute-start.6 = (f32[3,12,2,640]{3,1,2,0:T(8,128)S(1)}, f32[3,12,2,640]{3,1,2,0:T(8,128)S(1)}, u32[]{:S(2)}, u32[]{:S(2)}) collective-permute-start(f32[3,12,2,640]{3,1,2,0:T(8,128)S(1)} %copy.45), channel_id=1, source_target_pairs={{0,1},{1,2},{2,3},{4,5},{5,6},{6,7},{8,9},{9,10},{10,11},{12,13},{... | collective-permute-start | bytes 552968 | tf_op jit(solution)/shard_map/ppermute | solution.py:20
  127.1 6.9 %collective-permute-start.7 = (f32[3,12,2,640]{3,1,2,0:T(8,128)S(1)}, f32[3,12,2,640]{3,1,2,0:T(8,128)S(1)}, u32[]{:S(2)}, u32[]{:S(2)}) collective-permute-start(f32[3,12,2,640]{3,1,2,0:T(8,128)S(1)} %copy.46), channel_id=1, source_target_pairs={{1,0},{2,1},{3,2},{5,4},{6,5},{7,6},{9,8},{10,9},{11,10},{13,12},{... | collective-permute-start | bytes 552968 | tf_op jit(solution)/shard_map/ppermute | solution.py:21

commit v2 on v1

--- a/solution.py
+++ b/solution.py
@@ -8,19 +8,39 @@
 
 BOX_EPS = 1e-05
 SPREAD = (0.0625, 0.25, 0.375, 0.25, 0.0625)
+REACH = 4
+SPILL = 2
 
 
-def padded_2(x, sides, width):
-    for axis, dim in sides:
-        peers, length = (lax.axis_size(axis), x.shape[dim])
-        up = [(i, (i + 1) % peers) for i in range(peers - 1)]
-        down = [(j, i) for i, j in up]
-        last = lax.slice_in_dim(x, length - width, length, axis=dim)
-        initial = lax.slice_in_dim(x, 0, width, axis=dim)
-        before = lax.ppermute(last, axis, up)
-        after = lax.ppermute(initial, axis, down)
-        x = jnp.concatenate([before, x, after], axis=dim)
+def rim(x, side, dim, width):
+    length = x.shape[dim]
+    if side < 0:
+        return lax.slice_in_dim(x, length - width, length, axis=dim)
+    if side > 0:
+        return lax.slice_in_dim(x, 0, width, axis=dim)
     return x
+
+
+def halo_exchange(x, width):
+    nz, ny = (lax.axis_size("gz"), lax.axis_size("gy"))
+    grid = {}
+    for sz in (-1, 0, 1):
+        for sy in (-1, 0, 1):
+            if sz == 0 and sy == 0:
+                grid[sz, sy] = x
+                continue
+            piece = rim(rim(x, sz, 1, width), sy, 2, width)
+            perm = []
+            for gz in range(nz):
+                for gy in range(ny):
+                    tz, ty = (gz - sz, gy - sy)
+                    if 0 <= tz < nz and 0 <= ty < ny:
+                        perm.append((gz * ny + gy, tz * ny + ty))
+            grid[sz, sy] = lax.ppermute(piece, ("gz", "gy"), perm)
+    bands = [
+        jnp.concatenate([grid[sz, -1], grid[sz, 0], grid[sz, 1]], axis=2) for sz in (-1, 0, 1)
+    ]
+    return jnp.concatenate(bands, axis=1)
 
 
 def add_pair(former, latter):
@@ -73,7 +93,7 @@
     return (inside_z[:, :, None] & inside_y[:, None, :]).astype(jnp.float32)
 
 
-def subject_force(image_pad, templ_pad, region_mask, slab_depth, slab_rows):
+def subject_force(image_pad, templ_pad, region_mask, in_grid, slab_depth, slab_rows):
     templ_mean, templ_var = template_stats(templ_pad, slab_depth, slab_rows)
     mean_i = box_local(image_pad, slab_depth, slab_rows) / 729.0
     square_mean = box_local(image_pad * image_pad, slab_depth, slab_rows) / 729.0
@@ -99,18 +119,8 @@
     )
     side_pad = jnp.pad(image_mid, ((0, 0), (0, 0), (1, 1)))
     grad_x = 0.5 * (side_pad[:, :, 2:] - side_pad[:, :, :-2])
-    return jnp.stack([factor * grad_z, factor * grad_y, factor * grad_x])
-
-
-def scatter_sum(pieces, axis):
-    received = lax.all_to_all(pieces, axis, 0, 0, tiled=True)
-    return received
-
-
-def gather_all(part, axis):
-    peers = lax.axis_size(axis)
-    copies = jnp.broadcast_to(part[None], (peers,) + part.shape)
-    return lax.all_to_all(copies, axis, 0, 0, tiled=True)
+    force = jnp.stack([factor * grad_z, factor * grad_y, factor * grad_x])
+    return jnp.where(in_grid[None], force, 0.0)
 
 
 def local(subjects, templates, group_of, extents):
@@ -119,46 +129,58 @@
     peers = lax.axis_size("subj")
     cells = slab_depth * slab_rows * cell_count
     chunk = cells // peers
-    smoother = jax.vmap(partial(smooth_local, slab_depth=slab_depth, slab_rows=slab_rows))
+    depth_out, rows_out = (slab_depth + 2 * SPILL, slab_rows + 2 * SPILL)
+    total_z, total_y = (slab_depth * lax.axis_size("gz"), slab_rows * lax.axis_size("gy"))
     first_subject = lax.axis_index("subj") * local_subjects
     own_groups = lax.dynamic_slice_in_dim(group_of, first_subject, local_subjects)
     own_templates = jnp.take(templates, own_groups, axis=0)
-    z_index = lax.axis_index("gz") * slab_depth + jnp.arange(slab_depth, dtype=jnp.int32)
-    y_index = lax.axis_index("gy") * slab_rows + jnp.arange(slab_rows, dtype=jnp.int32)
+    z_start = lax.axis_index("gz") * slab_depth
+    y_start = lax.axis_index("gy") * slab_rows
+    z_index = z_start + jnp.arange(slab_depth, dtype=jnp.int32)
+    y_index = y_start + jnp.arange(slab_rows, dtype=jnp.int32)
     all_masks = region_masks(extents, z_index, y_index)
     own_masks = lax.dynamic_slice_in_dim(all_masks, first_subject, local_subjects)
     onehot = (group_of[:, None] == jnp.arange(groups, dtype=jnp.int32)[None, :]).astype(jnp.float32)
     counts = jnp.sum(onehot[:, :, None, None] * all_masks[:, None], axis=0)
     denominator = jnp.maximum(counts, 1.0)[..., None]
 
-    masked = own_masks[..., None] * subjects
-    pieces = masked.reshape(local_subjects, peers, chunk).transpose(1, 0, 2)
-    arrived = scatter_sum(pieces, "subj").reshape(peers * local_subjects, chunk)
-    group_parts = jnp.stack(
-        [
-            jnp.sum(jnp.where((group_of == g)[:, None], arrived, 0.0), axis=0)
-            for g in range(groups)
-        ]
+    z_wide = z_start - SPILL + jnp.arange(depth_out, dtype=jnp.int32)
+    y_wide = y_start - SPILL + jnp.arange(rows_out, dtype=jnp.int32)
+    wide_masks = lax.dynamic_slice_in_dim(
+        region_masks(extents, z_wide, y_wide), first_subject, local_subjects
     )
-    group_full = gather_all(group_parts, "subj")
-    template_sum = group_full.transpose(1, 0, 2).reshape(templates.shape)
-    new_templates = template_sum / denominator
+    in_grid = (
+        ((z_wide >= 0) & (z_wide < total_z))[:, None, None]
+        & ((y_wide >= 0) & (y_wide < total_y))[None, :, None]
+    )
 
     volumes = jnp.concatenate([own_templates, subjects], axis=0)
-    padded = padded_2(volumes, (("gz", 1), ("gy", 2)), 4)
+    padded = halo_exchange(volumes, REACH + SPILL)
     templ_all = padded[:local_subjects]
     image_all = padded[local_subjects:]
     forces = jax.vmap(
-        partial(subject_force, slab_depth=slab_depth, slab_rows=slab_rows)
-    )(image_all, templ_all, own_masks[..., None])
+        partial(subject_force, in_grid=in_grid, slab_depth=depth_out, slab_rows=rows_out)
+    )(image_all, templ_all, wide_masks[..., None])
     force_sum = jnp.sum(forces, axis=0)
+    smoother = jax.vmap(partial(smooth_local, slab_depth=slab_depth, slab_rows=slab_rows))
+    velocity_part = smoother(force_sum)
 
-    force_pieces = force_sum.reshape(3, peers, chunk).transpose(1, 0, 2)
-    force_part = jnp.sum(scatter_sum(force_pieces, "subj"), axis=0)
-    force_full = gather_all(force_part, "subj")
-    velocity_sum = force_full.transpose(1, 0, 2).reshape(3, slab_depth, slab_rows, cell_count)
-    summed_pad = padded_2(velocity_sum, (("gz", 1), ("gy", 2)), 2)
-    velocity = smoother(summed_pad)
+    masked = own_masks[..., None] * subjects
+    outgoing = jnp.concatenate(
+        [masked.reshape(local_subjects, peers, chunk), velocity_part.reshape(3, peers, chunk)]
+    ).transpose(1, 0, 2)
+    arrived = lax.all_to_all(outgoing, "subj", 0, 0, tiled=True)
+    images = arrived[:, :local_subjects].reshape(peers * local_subjects, chunk)
+    group_parts = [
+        jnp.sum(jnp.where((group_of == g)[:, None], images, 0.0), axis=0) for g in range(groups)
+    ]
+    velocity_chunk = jnp.sum(arrived[:, local_subjects:], axis=0)
+    reduced = jnp.concatenate([jnp.stack(group_parts), velocity_chunk])
+    copies = jnp.broadcast_to(reduced[None], (peers,) + reduced.shape)
+    gathered = lax.all_to_all(copies, "subj", 0, 0, tiled=True).transpose(1, 0, 2)
+    template_sum = gathered[:groups].reshape(templates.shape)
+    new_templates = template_sum / denominator
+    velocity = gathered[groups:].reshape(3, slab_depth, slab_rows, cell_count)
     return (new_templates, velocity)
 
 

time: 138 us -> 119 us (0.86)
  the two profiles are of different devices: /device:TPU:1 before, /device:TPU:32 now
where the time goes in v2:
time: 119 us
  starting transfers between devices  43.1 us (36%)
  waiting for transfers between devices  38 us (32%)
  other arithmetic  28.7 us (24%)
  local copies, waits for them, and re-layouts  5.99 us (5%)
  between operations  3.02 us (3%)
    ppermute x8, starting transfers between devices, halo_exchange(): grid[sz, sy] = lax.ppermute(piece, ('gz', 'gy'), perm)  30.8 us
    all_to_all x1, waiting for transfers between devices, local(): lax.all_to_all(copies, 'subj', 0, 0, tiled=True).transpose(1, 0, 2)  21.8 us
    add x11, other arithmetic, add_pair(): return former + latter  18.1 us
    all_to_all x1, waiting for transfers between devices, local(): arrived = lax.all_to_all(outgoing, 'subj', 0, 0, tiled=True)  12.6 us
    all_to_all x1, starting transfers between devices, local(): arrived = lax.all_to_all(outgoing, 'subj', 0, 0, tiled=True)  7.3 us
    all_to_all x1, starting transfers between devices, local(): lax.all_to_all(copies, 'subj', 0, 0, tiled=True).transpose(1, 0, 2)  4.92 us
    ppermute x8, waiting for transfers between devices, halo_exchange(): grid[sz, sy] = lax.ppermute(piece, ('gz', 'gy'), perm)  3.63 us
    another operation x3, other arithmetic, subject_force(): force = jnp.stack([factor * grad_z, factor * grad_y, factor * grad_x])  3.29 us
  transfers between devices with their start and end apart: 10, of which 3 were waited for; matrix products, arithmetic and copies ran while one was open for 1% of the time, Pallas kernels for 0%

profile of v2, /device:TPU:32, one launch (start us, length us, event | category | flops | bytes accessed | tf_op | source)
XLA Modules:
  0.0 118.8 jit_solution(3382522197810910312)
XLA Ops:
  0.6 1.3 %dynamic_slice.11 = s32[1]{0:T(128)} dynamic-slice(s32[16]{0:T(128)} %param.6, s32[]{:T(128)S(6)} %select_n.42), dynamic_slice_sizes={1} | dynamic-slice | bytes 12 | tf_op jit(solution)/shard_map/dynamic_slice | solution.py:135
  4.8 1.2 %fusion.85 = (f32[2,6,6,640]{3,2,1,0:T(8,128)S(1)}, f32[2,6,6,640]{3,2,1,0:T(8,128)S(1)}, f32[2,6,6,640]{3,2,1,0:T(8,128)S(1)}, f32[2,6,6,640]{3,2,1,0:T(8,128)S(1)}) fusion(f32[1,8,8,640]{3,2,1,0:T(8,128)S(1)} %dynamic-slice_select_fusion, f32[1,8,8,640]{3,2,1,0:T(8,128)} %param.4), kind=kLoop, calls=%fused_computation.243 | loop fusion | flops 184320 | bytes 1064960 | tf_op jit(solution)/shard_map/concatenate | solution.py:157
  6.0 1.3 %collective-permute-start.7 = (f32[2,6,6,640]{3,2,1,0:T(8,128)S(1)}, f32[2,6,6,640]{3,2,1,0:T(8,128)S(1)}, u32[]{:S(2)}, u32[]{:S(2)}) collective-permute-start(f32[2,6,6,640]{3,2,1,0:T(8,128)S(1)} %get-tuple-element.29), channel_id=1, source_target_pairs={{5,0},{6,1},{7,2},{9,4},{10,5},{11,6},{13,8},{14,9},{15,10},{21,16... | collective-permute-start | bytes 552968 | tf_op jit(solution)/shard_map/ppermute | solution.py:39
  8.1 1.3 %collective-permute-start.6 = (f32[2,6,8,640]{3,2,1,0:T(8,128)}, f32[2,6,8,640]{3,2,1,0:T(8,128)S(1)}, u32[]{:S(2)}, u32[]{:S(2)}) collective-permute-start(f32[2,6,8,640]{3,2,1,0:T(8,128)} %get-tuple-element.31), channel_id=1, source_target_pairs={{4,0},{5,1},{6,2},{7,3},{8,4},{9,5},{10,6},{11,7},{12,8},{13,9},{1... | collective-permute-start | bytes 737288 | tf_op jit(solution)/shard_map/ppermute | solution.py:39
  9.3 1.3 %collective-permute-start.5 = (f32[2,6,6,640]{3,2,1,0:T(8,128)S(1)}, f32[2,6,6,640]{3,2,1,0:T(8,128)}, u32[]{:S(2)}, u32[]{:S(2)}) collective-permute-start(f32[2,6,6,640]{3,2,1,0:T(8,128)S(1)} %get-tuple-element.28), channel_id=1, source_target_pairs={{4,1},{5,2},{6,3},{8,5},{9,6},{10,7},{12,9},{13,10},{14,11},{20,17... | collective-permute-start | bytes 552968 | tf_op jit(solution)/shard_map/ppermute | solution.py:39
  10.7 3.8 %collective-permute-start.4 = (f32[2,8,6,640]{3,2,1,0:T(8,128)S(1)}, f32[2,8,6,640]{3,2,1,0:T(8,128)S(1)}, u32[]{:S(2)}, u32[]{:S(2)}) collective-permute-start(f32[2,8,6,640]{3,2,1,0:T(8,128)S(1)} %get-tuple-element.33), channel_id=1, source_target_pairs={{1,0},{2,1},{3,2},{5,4},{6,5},{7,6},{9,8},{10,9},{11,10},{13,12},{... | collective-permute-start | bytes 737288 | tf_op jit(solution)/shard_map/ppermute | solution.py:39
  14.5 3.4 %collective-permute-start.2 = (f32[2,6,6,640]{3,2,1,0:T(8,128)S(1)}, f32[2,6,6,640]{3,2,1,0:T(8,128)}, u32[]{:S(2)}, u32[]{:S(2)}) collective-permute-start(f32[2,6,6,640]{3,2,1,0:T(8,128)S(1)} %get-tuple-element.27), channel_id=1, source_target_pairs={{1,4},{2,5},{3,6},{5,8},{6,9},{7,10},{9,12},{10,13},{11,14},{17,20... | collective-permute-start | bytes 552968 | tf_op jit(solution)/shard_map/ppermute | solution.py:39
  18.4 4.7 %collective-permute-start.3 = (f32[2,8,6,640]{3,2,1,0:T(8,128)S(1)}, f32[2,8,6,640]{3,2,1,0:T(8,128)S(1)}, u32[]{:S(2)}, u32[]{:S(2)}) collective-permute-start(f32[2,8,6,640]{3,2,1,0:T(8,128)S(1)} %get-tuple-element.32), channel_id=1, source_target_pairs={{0,1},{1,2},{2,3},{4,5},{5,6},{6,7},{8,9},{9,10},{10,11},{12,13},{... | collective-permute-start | bytes 737288 | tf_op jit(solution)/shard_map/ppermute | solution.py:39
  23.2 11.0 %collective-permute-start.1 = (f32[2,6,8,640]{3,2,1,0:T(8,128)S(1)}, f32[2,6,8,640]{3,2,1,0:T(8,128)}, u32[]{:S(2)}, u32[]{:S(2)}) collective-permute-start(f32[2,6,8,640]{3,2,1,0:T(8,128)S(1)} %get-tuple-element.30), channel_id=1, source_target_pairs={{0,4},{1,5},{2,6},{3,7},{4,8},{5,9},{6,10},{7,11},{8,12},{9,13},{1... | collective-permute-start | bytes 737288 | tf_op jit(solution)/shard_map/ppermute | solution.py:39
  34.2 4.1 %collective-permute-start = (f32[2,6,6,640]{3,2,1,0:T(8,128)S(1)}, f32[2,6,6,640]{3,2,1,0:T(8,128)S(1)}, u32[]{:S(2)}, u32[]{:S(2)}) collective-permute-start(f32[2,6,6,640]{3,2,1,0:T(8,128)S(1)} %get-tuple-element.26), channel_id=1, source_target_pairs={{0,5},{1,6},{2,7},{4,9},{5,10},{6,11},{8,13},{9,14},{10,15},{16,21... | collective-permute-start | bytes 552968 | tf_op jit(solution)/shard_map/ppermute | solution.py:39
  38.4 3.6 %collective-permute-done = f32[2,6,6,640]{3,2,1,0:T(8,128)S(1)} collective-permute-done((f32[2,6,6,640]{3,2,1,0:T(8,128)S(1)}, f32[2,6,6,640]{3,2,1,0:T(8,128)S(1)}, u32[]{:S(2)}, u32[]{:S(2)}) %collective-permute-start) | collective-permute-done | bytes 184352 | tf_op jit(solution)/shard_map/ppermute | solution.py:39
  42.0 1.7 %maximum_maximum_fusion = f32[2,20,20,640]{3,2,1,0:T(8,128)S(1)} fusion(f32[2,6,6,640]{3,2,1,0:T(8,128)S(1)} %collective-permute-done.7, f32[2,6,8,640]{3,2,1,0:T(8,128)S(1)} %collective-permute-done.6, f32[2,6,6,640]{3,2,1,0:T(8,128)} %collective-permute-done.5, f32[2,8,6,640]{3,2,1,0:T(8,128)S(1)} %collective-permute-done.4, f32[1,8,8,640]{3,2,1,0:T(8,128)S(1)} %copy-done, ...), kind=kLoop, calls=%fused_computation | loop fusion | flops 4608000 | bytes 4096000 | tf_op jit(solution)/shard_map/concatenate | solution.py:43
  44.2 2.6 %fusion.48 = f32[1,20,20,640]{3,2,1,0:T(8,128)S(1)} fusion(f32[1,20,20,640]{3,2,1,0:T(8,128)S(1)} %get-tuple-element.22), kind=kLoop, calls=%fused_computation.94 | loop fusion | flops 2048000 | bytes 2048000 | tf_op jit(solution)/shard_map/vmap()/add | solution.py:47
  47.4 5.2 %fusion.32 = (f32[1,20,20,640]{3,2,1,0:T(8,128)S(1)}, f32[1,20,20,640]{3,2,1,0:T(8,128)S(1)}) fusion(f32[1,20,20,640]{3,2,1,0:T(8,128)S(1)} %get-tuple-element.24, f32[1,20,20,640]{3,2,1,0:T(8,128)S(1)} %get-tuple-element.23), kind=kLoop, calls=%fused_computation.78 | loop fusion | flops 4096000 | bytes 4096000 | tf_op jit(solution)/shard_map/vmap()/add | solution.py:47
  53.8 5.2 %fusion.16 = (f32[1,20,20,640]{3,2,1,0:T(8,128)S(1)}, f32[1,20,20,640]{3,2,1,0:T(8,128)S(1)}) fusion(f32[1,20,20,640]{3,2,1,0:T(8,128)S(1)} %get-tuple-element.21, f32[1,20,20,640]{3,2,1,0:T(8,128)S(1)} %get-tuple-element.25), kind=kLoop, calls=%fused_computation.62 | loop fusion | flops 4096000 | bytes 4096000 | tf_op jit(solution)/shard_map/vmap()/add | solution.py:47
  60.2 2.8 %fusion.66 = (f32[1,1,12,12,640]{4,3,2,1,0:T(8,128)S(1)}, f32[1,12,12,640]{3,2,1,0:T(8,128)S(1)}) fusion(f32[2,20,20,640]{3,2,1,0:T(8,128)S(1)} %maximum_maximum_fusion, f32[1,20,12,640]{3,2,1,0:T(8,128)S(1)} %slice_add_fusion, f32[1,20,12,640]{3,2,1,0:T(8,128)S(1)} %slice_add_fusion.8, f32[1,20,12,640]{3,2,1,0:T(8,128)S(1)} %slice_add_fusion.16, ...), kind=kLoop, calls=%fused_computation.182 | loop fusion | flops 6082560 | bytes 18801216 | tf_op jit(solution)/shard_map/vmap()/stack | solution.py:122
  63.7 1.6 %fusion.4 = f32[3,12,12,640]{3,2,1,0:T(8,128)S(1)} fusion(f32[3,12,12,640]{3,2,1,0:T(8,128)S(1)} %fusion.8), kind=kLoop, calls=%fused_computation.49 | loop fusion | flops 2488320 | bytes 2211840 | tf_op jit(solution)/shard_map/vmap()/add | solution.py:47
  66.0 1.3 %copy.9 = f32[16,4,2560]{2,1,0:T(4,128)} copy(f32[16,4,2560]{2,0,1:T(8,128)S(1)} %maximum_bitcast_fusion.1) | data formatting | bytes 1310720 | tf_op jit(solution)/shard_map/transpose | solution.py:171
  67.3 7.3 %all-to-all-start = ((f32[16,4,2560]{2,1,0:T(4,128)}), f32[16,4,2560]{2,1,0:T(4,128)S(1)}, u32[]{:S(2)}, u32[]{:S(2)}) async-start(f32[16,4,2560]{2,1,0:T(4,128)} %copy.9), calls=%async_computation | async-start | bytes 1310720 | tf_op jit(solution)/shard_map/all_to_all | solution.py:172
  74.6 12.6 %all-to-all-done = f32[16,4,2560]{2,1,0:T(4,128)S(1)} async-done(((f32[16,4,2560]{2,1,0:T(4,128)}), f32[16,4,2560]{2,1,0:T(4,128)S(1)}, u32[]{:S(2)}, u32[]{:S(2)}) %all-to-all-start) | async-done | bytes 655392 | tf_op jit(solution)/shard_map/all_to_all | solution.py:172
  87.8 1.2 %broadcast_in_dim.96 = f32[16,7,2560]{2,1,0:T(8,128)} broadcast(f32[7,2560]{1,0:T(8,128)S(1)} %concatenate.27), dimensions={1,2} | broadcast | bytes 1218560 | tf_op jit(solution)/shard_map/broadcast_in_dim | solution.py:179
  89.0 4.9 %all-to-all-start.1 = ((f32[16,7,2560]{2,1,0:T(8,128)}), f32[16,7,2560]{2,1,0:T(8,128)S(1)}, u32[]{:S(2)}, u32[]{:S(2)}) async-start(f32[16,7,2560]{2,1,0:T(8,128)} %broadcast_in_dim.96), calls=%async_computation.1 | async-start | bytes 2621440 | tf_op jit(solution)/shard_map/all_to_all | solution.py:180
  94.2 21.8 %all-to-all-done.1 = f32[16,7,2560]{2,1,0:T(8,128)S(1)} async-done(((f32[16,7,2560]{2,1,0:T(8,128)}), f32[16,7,2560]{2,1,0:T(8,128)S(1)}, u32[]{:S(2)}, u32[]{:S(2)}) %all-to-all-start.1) | async-done | bytes 1146912 | tf_op jit(solution)/shard_map/all_to_all | solution.py:180
  117.8 1.0 broadcast_divide_fusion
  (64 shorter events, 9.6 us)
Async XLA Ops:
  0.6 6.7 %copy-start = (f32[1,8,8,640]{3,2,1,0:T(8,128)S(1)}, f32[1,8,8,640]{3,2,1,0:T(8,128)}, u32[]{:S(2)}) copy-start(f32[1,8,8,640]{3,2,1,0:T(8,128)} %param.4) | copy-start | bytes 491524
  6.0 11.9 %copy-start.2 = (s32[16,4]{0,1:T(4,128)S(1)}, s32[16,4]{0,1:T(4,128)}, u32[]{:S(2)}) copy-start(s32[16,4]{0,1:T(4,128)} %param.7) | copy-start | bytes 772
  6.0 12.4 %collective-permute-start.7 = (f32[2,6,6,640]{3,2,1,0:T(8,128)S(1)}, f32[2,6,6,640]{3,2,1,0:T(8,128)S(1)}, u32[]{:S(2)}, u32[]{:S(2)}) collective-permute-start(f32[2,6,6,640]{3,2,1,0:T(8,128)S(1)} %get-tuple-element.29), channel_id=1, source_target_pairs={{5,0},{6,1},{7,2},{9,4},{10,5},{11,6},{13,8},{14,9},{15,10},{21,16... | collective-permute-start | bytes 552968 | tf_op jit(solution)/shard_map/ppermute | solution.py:39
  8.1 33.9 %collective-permute-start.6 = (f32[2,6,8,640]{3,2,1,0:T(8,128)}, f32[2,6,8,640]{3,2,1,0:T(8,128)S(1)}, u32[]{:S(2)}, u32[]{:S(2)}) collective-permute-start(f32[2,6,8,640]{3,2,1,0:T(8,128)} %get-tuple-element.31), channel_id=1, source_target_pairs={{4,0},{5,1},{6,2},{7,3},{8,4},{9,5},{10,6},{11,7},{12,8},{13,9},{1... | collective-permute-start | bytes 737288 | tf_op jit(solution)/shard_map/ppermute | solution.py:39
  9.3 13.8 %collective-permute-start.5 = (f32[2,6,6,640]{3,2,1,0:T(8,128)S(1)}, f32[2,6,6,640]{3,2,1,0:T(8,128)}, u32[]{:S(2)}, u32[]{:S(2)}) collective-permute-start(f32[2,6,6,640]{3,2,1,0:T(8,128)S(1)} %get-tuple-element.28), channel_id=1, source_target_pairs={{4,1},{5,2},{6,3},{8,5},{9,6},{10,7},{12,9},{13,10},{14,11},{20,17... | collective-permute-start | bytes 552968 | tf_op jit(solution)/shard_map/ppermute | solution.py:39
  10.7 31.3 %collective-permute-start.4 = (f32[2,8,6,640]{3,2,1,0:T(8,128)S(1)}, f32[2,8,6,640]{3,2,1,0:T(8,128)S(1)}, u32[]{:S(2)}, u32[]{:S(2)}) collective-permute-start(f32[2,8,6,640]{3,2,1,0:T(8,128)S(1)} %get-tuple-element.33), channel_id=1, source_target_pairs={{1,0},{2,1},{3,2},{5,4},{6,5},{7,6},{9,8},{10,9},{11,10},{13,12},{... | collective-permute-start | bytes 737288 | tf_op jit(solution)/shard_map/ppermute | solution.py:39
  14.5 19.7 %collective-permute-start.2 = (f32[2,6,6,640]{3,2,1,0:T(8,128)S(1)}, f32[2,6,6,640]{3,2,1,0:T(8,128)}, u32[]{:S(2)}, u32[]{:S(2)}) collective-permute-start(f32[2,6,6,640]{3,2,1,0:T(8,128)S(1)} %get-tuple-element.27), channel_id=1, source_target_pairs={{1,4},{2,5},{3,6},{5,8},{6,9},{7,10},{9,12},{10,13},{11,14},{17,20... | collective-permute-start | bytes 552968 | tf_op jit(solution)/shard_map/ppermute | solution.py:39
  18.4 23.6 %collective-permute-start.3 = (f32[2,8,6,640]{3,2,1,0:T(8,128)S(1)}, f32[2,8,6,640]{3,2,1,0:T(8,128)S(1)}, u32[]{:S(2)}, u32[]{:S(2)}) collective-permute-start(f32[2,8,6,640]{3,2,1,0:T(8,128)S(1)} %get-tuple-element.32), channel_id=1, source_target_pairs={{0,1},{1,2},{2,3},{4,5},{5,6},{6,7},{8,9},{9,10},{10,11},{12,13},{... | collective-permute-start | bytes 737288 | tf_op jit(solution)/shard_map/ppermute | solution.py:39
  23.2 18.9 %collective-permute-start.1 = (f32[2,6,8,640]{3,2,1,0:T(8,128)S(1)}, f32[2,6,8,640]{3,2,1,0:T(8,128)}, u32[]{:S(2)}, u32[]{:S(2)}) collective-permute-start(f32[2,6,8,640]{3,2,1,0:T(8,128)S(1)} %get-tuple-element.30), channel_id=1, source_target_pairs={{0,4},{1,5},{2,6},{3,7},{4,8},{5,9},{6,10},{7,11},{8,12},{9,13},{1... | collective-permute-start | bytes 737288 | tf_op jit(solution)/shard_map/ppermute | solution.py:39
  34.2 7.8 %collective-permute-start = (f32[2,6,6,640]{3,2,1,0:T(8,128)S(1)}, f32[2,6,6,640]{3,2,1,0:T(8,128)S(1)}, u32[]{:S(2)}, u32[]{:S(2)}) collective-permute-start(f32[2,6,6,640]{3,2,1,0:T(8,128)S(1)} %get-tuple-element.26), channel_id=1, source_target_pairs={{0,5},{1,6},{2,7},{4,9},{5,10},{6,11},{8,13},{9,14},{10,15},{16,21... | collective-permute-start | bytes 552968 | tf_op jit(solution)/shard_map/ppermute | solution.py:39
  66.0 8.6 %copy-start.1 = (s32[16]{0:T(128)S(1)}, s32[16]{0:T(128)}, u32[]{:S(2)}) copy-start(s32[16]{0:T(128)} %param.6) | copy-start | bytes 196
  67.3 19.9 %all-to-all-start = ((f32[16,4,2560]{2,1,0:T(4,128)}), f32[16,4,2560]{2,1,0:T(4,128)S(1)}, u32[]{:S(2)}, u32[]{:S(2)}) async-start(f32[16,4,2560]{2,1,0:T(4,128)} %copy.9), calls=%async_computation | async-start | bytes 1310720 | tf_op jit(solution)/shard_map/all_to_all | solution.py:172
  89.0 27.0 %all-to-all-start.1 = ((f32[16,7,2560]{2,1,0:T(8,128)}), f32[16,7,2560]{2,1,0:T(8,128)S(1)}, u32[]{:S(2)}, u32[]{:S(2)}) async-start(f32[16,7,2560]{2,1,0:T(8,128)} %broadcast_in_dim.96), calls=%async_computation.1 | async-start | bytes 2621440 | tf_op jit(solution)/shard_map/all_to_all | solution.py:180

commit v3 on v2

--- a/solution.py
+++ b/solution.py
@@ -48,9 +48,14 @@
 
 
 def window_sum(volume, along_axis, length, extent):
+    inner = volume.shape[along_axis] - 2
+    triple = reduce(
+        add_pair,
+        [lax.slice_in_dim(volume, offset, offset + inner, axis=along_axis) for offset in range(3)],
+    )
     pieces = [
-        lax.slice_in_dim(volume, offset, offset + length, axis=along_axis)
-        for offset in range(extent)
+        lax.slice_in_dim(triple, offset, offset + length, axis=along_axis)
+        for offset in range(0, extent, 3)
     ]
     return reduce(add_pair, pieces)
 
@@ -154,8 +159,20 @@
         & ((y_wide >= 0) & (y_wide < total_y))[None, :, None]
     )
 
+    masked = own_masks[..., None] * subjects
+    outgoing = masked.reshape(local_subjects, peers, chunk).transpose(1, 0, 2)
+    arrived = lax.all_to_all(outgoing, "subj", 0, 0, tiled=True)
+    images = arrived.reshape(peers * local_subjects, chunk)
+    group_parts = jnp.stack(
+        [jnp.sum(jnp.where((group_of == g)[:, None], images, 0.0), axis=0) for g in range(groups)]
+    )
+    copies = jnp.broadcast_to(group_parts[None], (peers,) + group_parts.shape)
+    gathered = lax.all_to_all(copies, "subj", 0, 0, tiled=True).transpose(1, 0, 2)
+
     volumes = jnp.concatenate([own_templates, subjects], axis=0)
     padded = halo_exchange(volumes, REACH + SPILL)
+    gathered, padded = lax.optimization_barrier((gathered, padded))
+    new_templates = gathered.reshape(templates.shape) / denominator
     templ_all = padded[:local_subjects]
     image_all = padded[local_subjects:]
     forces = jax.vmap(
@@ -165,22 +182,11 @@
     smoother = jax.vmap(partial(smooth_local, slab_depth=slab_depth, slab_rows=slab_rows))
     velocity_part = smoother(force_sum)
 
-    masked = own_masks[..., None] * subjects
-    outgoing = jnp.concatenate(
-        [masked.reshape(local_subjects, peers, chunk), velocity_part.reshape(3, peers, chunk)]
-    ).transpose(1, 0, 2)
-    arrived = lax.all_to_all(outgoing, "subj", 0, 0, tiled=True)
-    images = arrived[:, :local_subjects].reshape(peers * local_subjects, chunk)
-    group_parts = [
-        jnp.sum(jnp.where((group_of == g)[:, None], images, 0.0), axis=0) for g in range(groups)
-    ]
-    velocity_chunk = jnp.sum(arrived[:, local_subjects:], axis=0)
-    reduced = jnp.concatenate([jnp.stack(group_parts), velocity_chunk])
-    copies = jnp.broadcast_to(reduced[None], (peers,) + reduced.shape)
+    outgoing = velocity_part.reshape(3, peers, chunk).transpose(1, 0, 2)
+    velocity_chunk = jnp.sum(lax.all_to_all(outgoing, "subj", 0, 0, tiled=True), axis=0)
+    copies = jnp.broadcast_to(velocity_chunk[None], (peers,) + velocity_chunk.shape)
     gathered = lax.all_to_all(copies, "subj", 0, 0, tiled=True).transpose(1, 0, 2)
-    template_sum = gathered[:groups].reshape(templates.shape)
-    new_templates = template_sum / denominator
-    velocity = gathered[groups:].reshape(3, slab_depth, slab_rows, cell_count)
+    velocity = gathered.reshape(3, slab_depth, slab_rows, cell_count)
     return (new_templates, velocity)
 
 

time: 119 us -> 121 us (1.017)
  the two profiles are of different devices: /device:TPU:32 before, /device:TPU:160 now
where the time goes in v3:
time: 121 us; the launch traced here: 120 us
  starting transfers between devices  44.7 us (37%)
  waiting for transfers between devices  41.4 us (34%)
  other arithmetic  22.7 us (19%)
  local copies, waits for them, and re-layouts  8.42 us (7%)
  between operations  3.16 us (3%)
    ppermute x8, starting transfers between devices, halo_exchange(): grid[sz, sy] = lax.ppermute(piece, ('gz', 'gy'), perm)  19.5 us
    ppermute x8, waiting for transfers between devices, halo_exchange(): grid[sz, sy] = lax.ppermute(piece, ('gz', 'gy'), perm)  18.2 us
    add x28, other arithmetic, add_pair(): return former + latter  14 us
    all_to_all x1, waiting for transfers between devices, local(): lax.all_to_all(outgoing, 'subj', 0, 0, tiled=True)  13.7 us
    all_to_all x2, starting transfers between devices, local(): lax.all_to_all(copies, 'subj', 0, 0, tiled=True).transpose(1, 0, 2)  10.9 us
    all_to_all x2, waiting for transfers between devices, local(): lax.all_to_all(copies, 'subj', 0, 0, tiled=True).transpose(1, 0, 2)  9.42 us
    all_to_all x1, starting transfers between devices, local(): lax.all_to_all(outgoing, 'subj', 0, 0, tiled=True)  7.21 us
    all_to_all x1, starting transfers between devices, local(): arrived = lax.all_to_all(outgoing, 'subj', 0, 0, tiled=True)  7.03 us
  transfers between devices with their start and end apart: 12, of which 3 were waited for; matrix products, arithmetic and copies ran while one was open for 7% of the time, Pallas kernels for 0%

profile of v3, /device:TPU:160, one launch (start us, length us, event | category | flops | bytes accessed | tf_op | source)
XLA Modules:
  0.0 120.3 jit_solution(7783699580695142850)
XLA Ops:
  3.5 7.0 %all-to-all-start = ((f32[16,1,2560]{2,1,0:T(1,128)}), f32[16,1,2560]{2,1,0:T(1,128)S(1)}, u32[]{:S(2)}, u32[]{:S(2)}) async-start(f32[16,1,2560]{2,1,0:T(1,128)} %transpose_reshape.3), calls=%async_computation | async-start | bytes 327680 | tf_op jit(solution)/shard_map/all_to_all | solution.py:164
  10.6 1.2 %dynamic_slice.10 = s32[1]{0:T(128)} dynamic-slice(s32[16]{0:T(128)} %param.6, s32[]{:T(128)S(6)} %select_n.42), dynamic_slice_sizes={1} | dynamic-slice | bytes 12 | tf_op jit(solution)/shard_map/dynamic_slice | solution.py:140
  14.8 1.9 %collective-permute-start.7 = (f32[2,6,6,640]{3,2,1,0:T(8,128)S(1)}, f32[2,6,6,640]{3,2,1,0:T(8,128)S(1)}, u32[]{:S(2)}, u32[]{:S(2)}) collective-permute-start(f32[2,6,6,640]{3,2,1,0:T(8,128)S(1)} %get-tuple-element.33), channel_id=1, source_target_pairs={{5,0},{6,1},{7,2},{9,4},{10,5},{11,6},{13,8},{14,9},{15,10},{21,16... | collective-permute-start | bytes 552968 | tf_op jit(solution)/shard_map/ppermute | solution.py:39
  17.5 1.9 %collective-permute-start.6 = (f32[2,6,8,640]{3,2,1,0:T(8,128)}, f32[2,6,8,640]{3,2,1,0:T(8,128)S(1)}, u32[]{:S(2)}, u32[]{:S(2)}) collective-permute-start(f32[2,6,8,640]{3,2,1,0:T(8,128)} %get-tuple-element.35), channel_id=1, source_target_pairs={{4,0},{5,1},{6,2},{7,3},{8,4},{9,5},{10,6},{11,7},{12,8},{13,9},{1... | collective-permute-start | bytes 737288 | tf_op jit(solution)/shard_map/ppermute | solution.py:39
  19.4 1.9 %collective-permute-start.5 = (f32[2,6,6,640]{3,2,1,0:T(8,128)S(1)}, f32[2,6,6,640]{3,2,1,0:T(8,128)}, u32[]{:S(2)}, u32[]{:S(2)}) collective-permute-start(f32[2,6,6,640]{3,2,1,0:T(8,128)S(1)} %get-tuple-element.32), channel_id=1, source_target_pairs={{4,1},{5,2},{6,3},{8,5},{9,6},{10,7},{12,9},{13,10},{14,11},{20,17... | collective-permute-start | bytes 552968 | tf_op jit(solution)/shard_map/ppermute | solution.py:39
  21.4 2.6 %collective-permute-start.4 = (f32[2,8,6,640]{3,2,1,0:T(8,128)S(1)}, f32[2,8,6,640]{3,2,1,0:T(8,128)S(1)}, u32[]{:S(2)}, u32[]{:S(2)}) collective-permute-start(f32[2,8,6,640]{3,2,1,0:T(8,128)S(1)} %get-tuple-element.37), channel_id=1, source_target_pairs={{1,0},{2,1},{3,2},{5,4},{6,5},{7,6},{9,8},{10,9},{11,10},{13,12},{... | collective-permute-start | bytes 737288 | tf_op jit(solution)/shard_map/ppermute | solution.py:39
  24.0 3.0 %collective-permute-start.2 = (f32[2,6,6,640]{3,2,1,0:T(8,128)S(1)}, f32[2,6,6,640]{3,2,1,0:T(8,128)}, u32[]{:S(2)}, u32[]{:S(2)}) collective-permute-start(f32[2,6,6,640]{3,2,1,0:T(8,128)S(1)} %get-tuple-element.31), channel_id=1, source_target_pairs={{1,4},{2,5},{3,6},{5,8},{6,9},{7,10},{9,12},{10,13},{11,14},{17,20... | collective-permute-start | bytes 552968 | tf_op jit(solution)/shard_map/ppermute | solution.py:39
  28.5 7.2 %all-to-all-start.1 = ((f32[16,4,2560]{2,1,0:T(4,128)}), f32[16,4,2560]{2,1,0:T(4,128)S(1)}, u32[]{:S(2)}, u32[]{:S(2)}) async-start(f32[16,4,2560]{2,1,0:T(4,128)} %broadcast_in_dim.97), calls=%async_computation.1 | async-start | bytes 1310720 | tf_op jit(solution)/shard_map/all_to_all | solution.py:170
  35.8 4.3 %collective-permute-start.3 = (f32[2,8,6,640]{3,2,1,0:T(8,128)S(1)}, f32[2,8,6,640]{3,2,1,0:T(8,128)S(1)}, u32[]{:S(2)}, u32[]{:S(2)}) collective-permute-start(f32[2,8,6,640]{3,2,1,0:T(8,128)S(1)} %get-tuple-element.36), channel_id=1, source_target_pairs={{0,1},{1,2},{2,3},{4,5},{5,6},{6,7},{8,9},{9,10},{10,11},{12,13},{... | collective-permute-start | bytes 737288 | tf_op jit(solution)/shard_map/ppermute | solution.py:39
  40.0 1.9 %collective-permute-start.1 = (f32[2,6,8,640]{3,2,1,0:T(8,128)}, f32[2,6,8,640]{3,2,1,0:T(8,128)S(1)}, u32[]{:S(2)}, u32[]{:S(2)}) collective-permute-start(f32[2,6,8,640]{3,2,1,0:T(8,128)} %get-tuple-element.34), channel_id=1, source_target_pairs={{0,4},{1,5},{2,6},{3,7},{4,8},{5,9},{6,10},{7,11},{8,12},{9,13},{1... | collective-permute-start | bytes 737288 | tf_op jit(solution)/shard_map/ppermute | solution.py:39
  42.0 1.9 %collective-permute-start = (f32[2,6,6,640]{3,2,1,0:T(8,128)S(1)}, f32[2,6,6,640]{3,2,1,0:T(8,128)S(1)}, u32[]{:S(2)}, u32[]{:S(2)}) collective-permute-start(f32[2,6,6,640]{3,2,1,0:T(8,128)S(1)} %get-tuple-element.30), channel_id=1, source_target_pairs={{0,5},{1,6},{2,7},{4,9},{5,10},{6,11},{8,13},{9,14},{10,15},{16,21... | collective-permute-start | bytes 552968 | tf_op jit(solution)/shard_map/ppermute | solution.py:39
  44.0 18.2 %collective-permute-done = f32[2,6,6,640]{3,2,1,0:T(8,128)S(1)} collective-permute-done((f32[2,6,6,640]{3,2,1,0:T(8,128)S(1)}, f32[2,6,6,640]{3,2,1,0:T(8,128)S(1)}, u32[]{:S(2)}, u32[]{:S(2)}) %collective-permute-start) | collective-permute-done | bytes 184352 | tf_op jit(solution)/shard_map/ppermute | solution.py:39
  63.0 2.1 %maximum_maximum_fusion = f32[2,20,20,640]{3,2,1,0:T(8,128)S(1)} fusion(f32[2,6,6,640]{3,2,1,0:T(8,128)} %copy-done.2, f32[2,6,8,640]{3,2,1,0:T(8,128)} %copy-done.3, f32[2,6,6,640]{3,2,1,0:T(8,128)} %collective-permute-done.5, f32[2,8,6,640]{3,2,1,0:T(8,128)} %copy-done.1, f32[1,8,8,640]{3,2,1,0:T(8,128)S(1)} %copy-done, ...), kind=kLoop, calls=%fused_computation | loop fusion | flops 4608000 | bytes 4096000 | tf_op jit(solution)/shard_map/concatenate | solution.py:43
  65.5 1.2 fusion.9
  67.9 1.2 fusion.7
  70.3 1.2 fusion.5
  72.7 1.2 fusion.3
  75.1 1.2 fusion.1
  79.1 1.6 %fusion.14 = f32[3,12,12,640]{3,2,1,0:T(8,128)S(1)} fusion(f32[3,12,12,640]{3,2,1,0:T(8,128)S(1)} %fusion.18), kind=kLoop, calls=%fused_computation.34 | loop fusion | flops 2488320 | bytes 2211840 | tf_op jit(solution)/shard_map/vmap()/add | solution.py:47
  81.4 1.2 copy.11
  82.5 7.2 %all-to-all-start.2 = ((f32[16,3,2560]{2,1,0:T(4,128)}), f32[16,3,2560]{2,1,0:T(4,128)S(1)}, u32[]{:S(2)}, u32[]{:S(2)}) async-start(f32[16,3,2560]{2,1,0:T(4,128)} %copy.11), calls=%async_computation.2 | async-start | bytes 1310720 | tf_op jit(solution)/shard_map/all_to_all | solution.py:186
  90.0 13.7 %all-to-all-done.2 = f32[16,3,2560]{2,1,0:T(4,128)S(1)} async-done(((f32[16,3,2560]{2,1,0:T(4,128)}), f32[16,3,2560]{2,1,0:T(4,128)S(1)}, u32[]{:S(2)}, u32[]{:S(2)}) %all-to-all-start.2) | async-done | bytes 491552 | tf_op jit(solution)/shard_map/all_to_all | solution.py:186
  104.7 3.7 %all-to-all-start.3 = ((f32[16,3,2560]{2,1,0:T(4,128)}), f32[16,3,2560]{2,1,0:T(4,128)S(1)}, u32[]{:S(2)}, u32[]{:S(2)}) async-start(f32[16,3,2560]{2,1,0:T(4,128)} %broadcast_in_dim.103), calls=%async_computation.3 | async-start | bytes 1310720 | tf_op jit(solution)/shard_map/all_to_all | solution.py:188
  109.8 9.4 %all-to-all-done.3 = f32[16,3,2560]{2,1,0:T(4,128)S(1)} async-done(((f32[16,3,2560]{2,1,0:T(4,128)}), f32[16,3,2560]{2,1,0:T(4,128)S(1)}, u32[]{:S(2)}, u32[]{:S(2)}) %all-to-all-start.3) | async-done | bytes 491552 | tf_op jit(solution)/shard_map/all_to_all | solution.py:188
  (86 shorter events, 19.1 us)
Async XLA Ops:
  0.6 14.1 %copy-start = (f32[1,8,8,640]{3,2,1,0:T(8,128)S(1)}, f32[1,8,8,640]{3,2,1,0:T(8,128)}, u32[]{:S(2)}) copy-start(f32[1,8,8,640]{3,2,1,0:T(8,128)} %param.4) | copy-start | bytes 491524
  3.5 23.8 %all-to-all-start = ((f32[16,1,2560]{2,1,0:T(1,128)}), f32[16,1,2560]{2,1,0:T(1,128)S(1)}, u32[]{:S(2)}, u32[]{:S(2)}) async-start(f32[16,1,2560]{2,1,0:T(1,128)} %transpose_reshape.3), calls=%async_computation | async-start | bytes 327680 | tf_op jit(solution)/shard_map/all_to_all | solution.py:164
  14.7 12.6 %copy-start.4 = (s32[16]{0:T(128)S(1)}, s32[16]{0:T(128)}, u32[]{:S(2)}) copy-start(s32[16]{0:T(128)} %param.6) | copy-start | bytes 196
  14.8 21.0 %collective-permute-start.7 = (f32[2,6,6,640]{3,2,1,0:T(8,128)S(1)}, f32[2,6,6,640]{3,2,1,0:T(8,128)S(1)}, u32[]{:S(2)}, u32[]{:S(2)}) collective-permute-start(f32[2,6,6,640]{3,2,1,0:T(8,128)S(1)} %get-tuple-element.33), channel_id=1, source_target_pairs={{5,0},{6,1},{7,2},{9,4},{10,5},{11,6},{13,8},{14,9},{15,10},{21,16... | collective-permute-start | bytes 552968 | tf_op jit(solution)/shard_map/ppermute | solution.py:39
  17.5 44.7 %collective-permute-start.6 = (f32[2,6,8,640]{3,2,1,0:T(8,128)}, f32[2,6,8,640]{3,2,1,0:T(8,128)S(1)}, u32[]{:S(2)}, u32[]{:S(2)}) collective-permute-start(f32[2,6,8,640]{3,2,1,0:T(8,128)} %get-tuple-element.35), channel_id=1, source_target_pairs={{4,0},{5,1},{6,2},{7,3},{8,4},{9,5},{10,6},{11,7},{12,8},{13,9},{1... | collective-permute-start | bytes 737288 | tf_op jit(solution)/shard_map/ppermute | solution.py:39
  19.4 20.6 %collective-permute-start.5 = (f32[2,6,6,640]{3,2,1,0:T(8,128)S(1)}, f32[2,6,6,640]{3,2,1,0:T(8,128)}, u32[]{:S(2)}, u32[]{:S(2)}) collective-permute-start(f32[2,6,6,640]{3,2,1,0:T(8,128)S(1)} %get-tuple-element.32), channel_id=1, source_target_pairs={{4,1},{5,2},{6,3},{8,5},{9,6},{10,7},{12,9},{13,10},{14,11},{20,17... | collective-permute-start | bytes 552968 | tf_op jit(solution)/shard_map/ppermute | solution.py:39
  21.4 40.8 %collective-permute-start.4 = (f32[2,8,6,640]{3,2,1,0:T(8,128)S(1)}, f32[2,8,6,640]{3,2,1,0:T(8,128)S(1)}, u32[]{:S(2)}, u32[]{:S(2)}) collective-permute-start(f32[2,8,6,640]{3,2,1,0:T(8,128)S(1)} %get-tuple-element.37), channel_id=1, source_target_pairs={{1,0},{2,1},{3,2},{5,4},{6,5},{7,6},{9,8},{10,9},{11,10},{13,12},{... | collective-permute-start | bytes 737288 | tf_op jit(solution)/shard_map/ppermute | solution.py:39
  24.0 18.0 %collective-permute-start.2 = (f32[2,6,6,640]{3,2,1,0:T(8,128)S(1)}, f32[2,6,6,640]{3,2,1,0:T(8,128)}, u32[]{:S(2)}, u32[]{:S(2)}) collective-permute-start(f32[2,6,6,640]{3,2,1,0:T(8,128)S(1)} %get-tuple-element.31), channel_id=1, source_target_pairs={{1,4},{2,5},{3,6},{5,8},{6,9},{7,10},{9,12},{10,13},{11,14},{17,20... | collective-permute-start | bytes 552968 | tf_op jit(solution)/shard_map/ppermute | solution.py:39
  28.5 36.6 %all-to-all-start.1 = ((f32[16,4,2560]{2,1,0:T(4,128)}), f32[16,4,2560]{2,1,0:T(4,128)S(1)}, u32[]{:S(2)}, u32[]{:S(2)}) async-start(f32[16,4,2560]{2,1,0:T(4,128)} %broadcast_in_dim.97), calls=%async_computation.1 | async-start | bytes 1310720 | tf_op jit(solution)/shard_map/all_to_all | solution.py:170
  35.7 26.5 %copy-start.2 = (f32[2,6,6,640]{3,2,1,0:T(8,128)}, f32[2,6,6,640]{3,2,1,0:T(8,128)S(1)}, u32[]{:S(2)}) copy-start(f32[2,6,6,640]{3,2,1,0:T(8,128)S(1)} %collective-permute-done.7) | copy-start | bytes 552964
  35.8 26.5 %collective-permute-start.3 = (f32[2,8,6,640]{3,2,1,0:T(8,128)S(1)}, f32[2,8,6,640]{3,2,1,0:T(8,128)S(1)}, u32[]{:S(2)}, u32[]{:S(2)}) collective-permute-start(f32[2,8,6,640]{3,2,1,0:T(8,128)S(1)} %get-tuple-element.36), channel_id=1, source_target_pairs={{0,1},{1,2},{2,3},{4,5},{5,6},{6,7},{8,9},{9,10},{10,11},{12,13},{... | collective-permute-start | bytes 737288 | tf_op jit(solution)/shard_map/ppermute | solution.py:39
  40.0 23.0 %collective-permute-start.1 = (f32[2,6,8,640]{3,2,1,0:T(8,128)}, f32[2,6,8,640]{3,2,1,0:T(8,128)S(1)}, u32[]{:S(2)}, u32[]{:S(2)}) collective-permute-start(f32[2,6,8,640]{3,2,1,0:T(8,128)} %get-tuple-element.34), channel_id=1, source_target_pairs={{0,4},{1,5},{2,6},{3,7},{4,8},{5,9},{6,10},{7,11},{8,12},{9,13},{1... | collective-permute-start | bytes 737288 | tf_op jit(solution)/shard_map/ppermute | solution.py:39
  42.0 20.2 %collective-permute-start = (f32[2,6,6,640]{3,2,1,0:T(8,128)S(1)}, f32[2,6,6,640]{3,2,1,0:T(8,128)S(1)}, u32[]{:S(2)}, u32[]{:S(2)}) collective-permute-start(f32[2,6,6,640]{3,2,1,0:T(8,128)S(1)} %get-tuple-element.30), channel_id=1, source_target_pairs={{0,5},{1,6},{2,7},{4,9},{5,10},{6,11},{8,13},{9,14},{10,15},{16,21... | collective-permute-start | bytes 552968 | tf_op jit(solution)/shard_map/ppermute | solution.py:39
  62.2 0.7 copy-start.3
  62.2 0.8 copy-start.1
  82.5 21.2 %all-to-all-start.2 = ((f32[16,3,2560]{2,1,0:T(4,128)}), f32[16,3,2560]{2,1,0:T(4,128)S(1)}, u32[]{:S(2)}, u32[]{:S(2)}) async-start(f32[16,3,2560]{2,1,0:T(4,128)} %copy.11), calls=%async_computation.2 | async-start | bytes 1310720 | tf_op jit(solution)/shard_map/all_to_all | solution.py:186
  104.7 14.5 %all-to-all-start.3 = ((f32[16,3,2560]{2,1,0:T(4,128)}), f32[16,3,2560]{2,1,0:T(4,128)S(1)}, u32[]{:S(2)}, u32[]{:S(2)}) async-start(f32[16,3,2560]{2,1,0:T(4,128)} %broadcast_in_dim.103), calls=%async_computation.3 | async-start | bytes 1310720 | tf_op jit(solution)/shard_map/all_to_all | solution.py:188

commit v4 on v3

--- a/solution.py
+++ b/solution.py
@@ -128,7 +128,7 @@
     return jnp.where(in_grid[None], force, 0.0)
 
 
-def local(subjects, templates, group_of, extents):
+def step(subjects, templates, group_of, extents):
     local_subjects, slab_depth, slab_rows, cell_count = subjects.shape
     groups = templates.shape[0]
     peers = lax.axis_size("subj")
@@ -159,15 +159,14 @@
         & ((y_wide >= 0) & (y_wide < total_y))[None, :, None]
     )
 
-    masked = own_masks[..., None] * subjects
-    outgoing = masked.reshape(local_subjects, peers, chunk).transpose(1, 0, 2)
-    arrived = lax.all_to_all(outgoing, "subj", 0, 0, tiled=True)
-    images = arrived.reshape(peers * local_subjects, chunk)
+    masked = (own_masks[..., None] * subjects).reshape(local_subjects, peers, chunk)
+    arrived = lax.all_to_all(masked, "subj", 1, 1, tiled=True)
+    images = arrived.transpose(1, 0, 2).reshape(peers * local_subjects, chunk)
     group_parts = jnp.stack(
         [jnp.sum(jnp.where((group_of == g)[:, None], images, 0.0), axis=0) for g in range(groups)]
     )
-    copies = jnp.broadcast_to(group_parts[None], (peers,) + group_parts.shape)
-    gathered = lax.all_to_all(copies, "subj", 0, 0, tiled=True).transpose(1, 0, 2)
+    copies = jnp.broadcast_to(group_parts[:, None], (groups, peers, chunk))
+    gathered = lax.all_to_all(copies, "subj", 1, 1, tiled=True)
 
     volumes = jnp.concatenate([own_templates, subjects], axis=0)
     padded = halo_exchange(volumes, REACH + SPILL)
@@ -180,12 +179,11 @@
     )(image_all, templ_all, wide_masks[..., None])
     force_sum = jnp.sum(forces, axis=0)
     smoother = jax.vmap(partial(smooth_local, slab_depth=slab_depth, slab_rows=slab_rows))
-    velocity_part = smoother(force_sum)
+    velocity_part = smoother(force_sum).reshape(3, peers, chunk)
 
-    outgoing = velocity_part.reshape(3, peers, chunk).transpose(1, 0, 2)
-    velocity_chunk = jnp.sum(lax.all_to_all(outgoing, "subj", 0, 0, tiled=True), axis=0)
-    copies = jnp.broadcast_to(velocity_chunk[None], (peers,) + velocity_chunk.shape)
-    gathered = lax.all_to_all(copies, "subj", 0, 0, tiled=True).transpose(1, 0, 2)
+    velocity_chunk = jnp.sum(lax.all_to_all(velocity_part, "subj", 1, 1, tiled=True), axis=1)
+    copies = jnp.broadcast_to(velocity_chunk[:, None], (3, peers, chunk))
+    gathered = lax.all_to_all(copies, "subj", 1, 1, tiled=True)
     velocity = gathered.reshape(3, slab_depth, slab_rows, cell_count)
     return (new_templates, velocity)
 
@@ -193,4 +191,4 @@
 def solution(mesh):
     in_specs = (P("subj", "gz", "gy", None), P(None, "gz", "gy", None), P(), P())
     out_specs = (P(None, "gz", "gy", None), P(None, "gz", "gy", None))
-    return jax.shard_map(local, mesh=mesh, in_specs=in_specs, out_specs=out_specs, check_vma=False)
+    return jax.shard_map(step, mesh=mesh, in_specs=in_specs, out_specs=out_specs, check_vma=False)

time: 121 us -> 121 us (level)
    reshape x3 -> x5, local copies, waits for them, and re-layouts: 1.18 us -> 3.18 us  [the longest x2 1.25 us: step(): velocity_part = smoother(force_sum).reshape(3, peers, chunk)]
    transpose x2 -> x0, local copies, waits for them, and re-layouts: 1.34 us -> none  [the longest x1 1.18 us: local(): outgoing = velocity_part.reshape(3, peers, chunk).transpose(1, 0, 2)]
where the time goes in v4:
time: 121 us; the launch traced here: 120 us
  starting transfers between devices  44.7 us (37%)
  waiting for transfers between devices  41.4 us (34%)
  other arithmetic  22.7 us (19%)
  local copies, waits for them, and re-layouts  8.42 us (7%)
  between operations  3.16 us (3%)
    ppermute x8, starting transfers between devices, halo_exchange(): grid[sz, sy] = lax.ppermute(piece, ('gz', 'gy'), perm)  19.5 us
    ppermute x8, waiting for transfers between devices, halo_exchange(): grid[sz, sy] = lax.ppermute(piece, ('gz', 'gy'), perm)  18.2 us
    add x28, other arithmetic, add_pair(): return former + latter  14 us
    all_to_all x1, waiting for transfers between devices, step(): lax.all_to_all(velocity_part, 'subj', 1, 1, tiled=True)  13.7 us
    all_to_all x2, starting transfers between devices, step(): gathered = lax.all_to_all(copies, 'subj', 1, 1, tiled=True)  10.9 us
    all_to_all x2, waiting for transfers between devices, step(): gathered = lax.all_to_all(copies, 'subj', 1, 1, tiled=True)  9.42 us
    all_to_all x1, starting transfers between devices, step(): lax.all_to_all(velocity_part, 'subj', 1, 1, tiled=True)  7.21 us
    all_to_all x1, starting transfers between devices, step(): arrived = lax.all_to_all(masked, 'subj', 1, 1, tiled=True)  7.03 us
  transfers between devices with their start and end apart: 12, of which 3 were waited for; matrix products, arithmetic and copies ran while one was open for 7% of the time, Pallas kernels for 0%

profile of v4, /device:TPU:160, one launch (start us, length us, event | category | flops | bytes accessed | tf_op | source)
XLA Modules:
  0.0 120.3 jit_solution(6413818012122489605)
XLA Ops:
  3.5 7.0 %all-to-all-start = ((f32[1,16,2560]{2,0,1:T(1,128)}), f32[1,16,2560]{2,0,1:T(1,128)S(1)}, u32[]{:S(2)}, u32[]{:S(2)}) async-start(f32[1,16,2560]{2,0,1:T(1,128)} %reshape.352), calls=%async_computation | async-start | bytes 327680 | tf_op jit(solution)/shard_map/all_to_all | solution.py:163
  10.6 1.2 %dynamic_slice.10 = s32[1]{0:T(128)} dynamic-slice(s32[16]{0:T(128)} %param.6, s32[]{:T(128)S(6)} %select_n.42), dynamic_slice_sizes={1} | dynamic-slice | bytes 12 | tf_op jit(solution)/shard_map/dynamic_slice | solution.py:140
  14.8 1.9 %collective-permute-start.7 = (f32[2,6,6,640]{3,2,1,0:T(8,128)S(1)}, f32[2,6,6,640]{3,2,1,0:T(8,128)S(1)}, u32[]{:S(2)}, u32[]{:S(2)}) collective-permute-start(f32[2,6,6,640]{3,2,1,0:T(8,128)S(1)} %get-tuple-element.33), channel_id=1, source_target_pairs={{5,0},{6,1},{7,2},{9,4},{10,5},{11,6},{13,8},{14,9},{15,10},{21,16... | collective-permute-start | bytes 552968 | tf_op jit(solution)/shard_map/ppermute | solution.py:39
  17.5 1.9 %collective-permute-start.6 = (f32[2,6,8,640]{3,2,1,0:T(8,128)}, f32[2,6,8,640]{3,2,1,0:T(8,128)S(1)}, u32[]{:S(2)}, u32[]{:S(2)}) collective-permute-start(f32[2,6,8,640]{3,2,1,0:T(8,128)} %get-tuple-element.35), channel_id=1, source_target_pairs={{4,0},{5,1},{6,2},{7,3},{8,4},{9,5},{10,6},{11,7},{12,8},{13,9},{1... | collective-permute-start | bytes 737288 | tf_op jit(solution)/shard_map/ppermute | solution.py:39
  19.4 1.9 %collective-permute-start.5 = (f32[2,6,6,640]{3,2,1,0:T(8,128)S(1)}, f32[2,6,6,640]{3,2,1,0:T(8,128)}, u32[]{:S(2)}, u32[]{:S(2)}) collective-permute-start(f32[2,6,6,640]{3,2,1,0:T(8,128)S(1)} %get-tuple-element.32), channel_id=1, source_target_pairs={{4,1},{5,2},{6,3},{8,5},{9,6},{10,7},{12,9},{13,10},{14,11},{20,17... | collective-permute-start | bytes 552968 | tf_op jit(solution)/shard_map/ppermute | solution.py:39
  21.4 2.6 %collective-permute-start.4 = (f32[2,8,6,640]{3,2,1,0:T(8,128)S(1)}, f32[2,8,6,640]{3,2,1,0:T(8,128)S(1)}, u32[]{:S(2)}, u32[]{:S(2)}) collective-permute-start(f32[2,8,6,640]{3,2,1,0:T(8,128)S(1)} %get-tuple-element.37), channel_id=1, source_target_pairs={{1,0},{2,1},{3,2},{5,4},{6,5},{7,6},{9,8},{10,9},{11,10},{13,12},{... | collective-permute-start | bytes 737288 | tf_op jit(solution)/shard_map/ppermute | solution.py:39
  24.0 3.0 %collective-permute-start.2 = (f32[2,6,6,640]{3,2,1,0:T(8,128)S(1)}, f32[2,6,6,640]{3,2,1,0:T(8,128)}, u32[]{:S(2)}, u32[]{:S(2)}) collective-permute-start(f32[2,6,6,640]{3,2,1,0:T(8,128)S(1)} %get-tuple-element.31), channel_id=1, source_target_pairs={{1,4},{2,5},{3,6},{5,8},{6,9},{7,10},{9,12},{10,13},{11,14},{17,20... | collective-permute-start | bytes 552968 | tf_op jit(solution)/shard_map/ppermute | solution.py:39
  28.5 7.2 %all-to-all-start.1 = ((f32[4,16,2560]{2,0,1:T(4,128)}), f32[4,16,2560]{2,0,1:T(4,128)S(1)}, u32[]{:S(2)}, u32[]{:S(2)}) async-start(f32[4,16,2560]{2,0,1:T(4,128)} %broadcast_in_dim.97), calls=%async_computation.1 | async-start | bytes 1310720 | tf_op jit(solution)/shard_map/all_to_all | solution.py:169
  35.8 4.3 %collective-permute-start.3 = (f32[2,8,6,640]{3,2,1,0:T(8,128)S(1)}, f32[2,8,6,640]{3,2,1,0:T(8,128)S(1)}, u32[]{:S(2)}, u32[]{:S(2)}) collective-permute-start(f32[2,8,6,640]{3,2,1,0:T(8,128)S(1)} %get-tuple-element.36), channel_id=1, source_target_pairs={{0,1},{1,2},{2,3},{4,5},{5,6},{6,7},{8,9},{9,10},{10,11},{12,13},{... | collective-permute-start | bytes 737288 | tf_op jit(solution)/shard_map/ppermute | solution.py:39
  40.0 1.9 %collective-permute-start.1 = (f32[2,6,8,640]{3,2,1,0:T(8,128)}, f32[2,6,8,640]{3,2,1,0:T(8,128)S(1)}, u32[]{:S(2)}, u32[]{:S(2)}) collective-permute-start(f32[2,6,8,640]{3,2,1,0:T(8,128)} %get-tuple-element.34), channel_id=1, source_target_pairs={{0,4},{1,5},{2,6},{3,7},{4,8},{5,9},{6,10},{7,11},{8,12},{9,13},{1... | collective-permute-start | bytes 737288 | tf_op jit(solution)/shard_map/ppermute | solution.py:39
  42.0 1.9 %collective-permute-start = (f32[2,6,6,640]{3,2,1,0:T(8,128)S(1)}, f32[2,6,6,640]{3,2,1,0:T(8,128)S(1)}, u32[]{:S(2)}, u32[]{:S(2)}) collective-permute-start(f32[2,6,6,640]{3,2,1,0:T(8,128)S(1)} %get-tuple-element.30), channel_id=1, source_target_pairs={{0,5},{1,6},{2,7},{4,9},{5,10},{6,11},{8,13},{9,14},{10,15},{16,21... | collective-permute-start | bytes 552968 | tf_op jit(solution)/shard_map/ppermute | solution.py:39
  44.0 18.2 %collective-permute-done = f32[2,6,6,640]{3,2,1,0:T(8,128)S(1)} collective-permute-done((f32[2,6,6,640]{3,2,1,0:T(8,128)S(1)}, f32[2,6,6,640]{3,2,1,0:T(8,128)S(1)}, u32[]{:S(2)}, u32[]{:S(2)}) %collective-permute-start) | collective-permute-done | bytes 184352 | tf_op jit(solution)/shard_map/ppermute | solution.py:39
  63.0 2.1 %maximum_maximum_fusion = f32[2,20,20,640]{3,2,1,0:T(8,128)S(1)} fusion(f32[2,6,6,640]{3,2,1,0:T(8,128)} %copy-done.2, f32[2,6,8,640]{3,2,1,0:T(8,128)} %copy-done.3, f32[2,6,6,640]{3,2,1,0:T(8,128)} %collective-permute-done.5, f32[2,8,6,640]{3,2,1,0:T(8,128)} %copy-done.1, f32[1,8,8,640]{3,2,1,0:T(8,128)S(1)} %copy-done, ...), kind=kLoop, calls=%fused_computation | loop fusion | flops 4608000 | bytes 4096000 | tf_op jit(solution)/shard_map/concatenate | solution.py:43
  65.5 1.2 fusion.9
  67.9 1.2 fusion.7
  70.3 1.2 fusion.5
  72.7 1.2 fusion.3
  75.1 1.2 fusion.1
  79.1 1.6 %fusion.14 = f32[3,12,12,640]{3,2,1,0:T(8,128)S(1)} fusion(f32[3,12,12,640]{3,2,1,0:T(8,128)S(1)} %fusion.18), kind=kLoop, calls=%fused_computation.34 | loop fusion | flops 2488320 | bytes 2211840 | tf_op jit(solution)/shard_map/vmap()/add | solution.py:47
  81.4 1.2 copy.11
  82.5 7.2 %all-to-all-start.2 = ((f32[3,16,2560]{2,0,1:T(4,128)}), f32[3,16,2560]{2,0,1:T(4,128)S(1)}, u32[]{:S(2)}, u32[]{:S(2)}) async-start(f32[3,16,2560]{2,0,1:T(4,128)} %copy.11), calls=%async_computation.2 | async-start | bytes 1310720 | tf_op jit(solution)/shard_map/all_to_all | solution.py:184
  90.0 13.7 %all-to-all-done.2 = f32[3,16,2560]{2,0,1:T(4,128)S(1)} async-done(((f32[3,16,2560]{2,0,1:T(4,128)}), f32[3,16,2560]{2,0,1:T(4,128)S(1)}, u32[]{:S(2)}, u32[]{:S(2)}) %all-to-all-start.2) | async-done | bytes 491552 | tf_op jit(solution)/shard_map/all_to_all | solution.py:184
  104.7 3.7 %all-to-all-start.3 = ((f32[3,16,2560]{2,0,1:T(4,128)}), f32[3,16,2560]{2,0,1:T(4,128)S(1)}, u32[]{:S(2)}, u32[]{:S(2)}) async-start(f32[3,16,2560]{2,0,1:T(4,128)} %broadcast_in_dim.103), calls=%async_computation.3 | async-start | bytes 1310720 | tf_op jit(solution)/shard_map/all_to_all | solution.py:186
  109.8 9.4 %all-to-all-done.3 = f32[3,16,2560]{2,0,1:T(4,128)S(1)} async-done(((f32[3,16,2560]{2,0,1:T(4,128)}), f32[3,16,2560]{2,0,1:T(4,128)S(1)}, u32[]{:S(2)}, u32[]{:S(2)}) %all-to-all-start.3) | async-done | bytes 491552 | tf_op jit(solution)/shard_map/all_to_all | solution.py:186
  (86 shorter events, 19.1 us)
Async XLA Ops:
  0.6 14.1 %copy-start = (f32[1,8,8,640]{3,2,1,0:T(8,128)S(1)}, f32[1,8,8,640]{3,2,1,0:T(8,128)}, u32[]{:S(2)}) copy-start(f32[1,8,8,640]{3,2,1,0:T(8,128)} %param.4) | copy-start | bytes 491524
  3.5 23.8 %all-to-all-start = ((f32[1,16,2560]{2,0,1:T(1,128)}), f32[1,16,2560]{2,0,1:T(1,128)S(1)}, u32[]{:S(2)}, u32[]{:S(2)}) async-start(f32[1,16,2560]{2,0,1:T(1,128)} %reshape.352), calls=%async_computation | async-start | bytes 327680 | tf_op jit(solution)/shard_map/all_to_all | solution.py:163
  14.7 12.6 %copy-start.4 = (s32[16]{0:T(128)S(1)}, s32[16]{0:T(128)}, u32[]{:S(2)}) copy-start(s32[16]{0:T(128)} %param.6) | copy-start | bytes 196
  14.8 21.0 %collective-permute-start.7 = (f32[2,6,6,640]{3,2,1,0:T(8,128)S(1)}, f32[2,6,6,640]{3,2,1,0:T(8,128)S(1)}, u32[]{:S(2)}, u32[]{:S(2)}) collective-permute-start(f32[2,6,6,640]{3,2,1,0:T(8,128)S(1)} %get-tuple-element.33), channel_id=1, source_target_pairs={{5,0},{6,1},{7,2},{9,4},{10,5},{11,6},{13,8},{14,9},{15,10},{21,16... | collective-permute-start | bytes 552968 | tf_op jit(solution)/shard_map/ppermute | solution.py:39
  17.5 44.7 %collective-permute-start.6 = (f32[2,6,8,640]{3,2,1,0:T(8,128)}, f32[2,6,8,640]{3,2,1,0:T(8,128)S(1)}, u32[]{:S(2)}, u32[]{:S(2)}) collective-permute-start(f32[2,6,8,640]{3,2,1,0:T(8,128)} %get-tuple-element.35), channel_id=1, source_target_pairs={{4,0},{5,1},{6,2},{7,3},{8,4},{9,5},{10,6},{11,7},{12,8},{13,9},{1... | collective-permute-start | bytes 737288 | tf_op jit(solution)/shard_map/ppermute | solution.py:39
  19.4 20.6 %collective-permute-start.5 = (f32[2,6,6,640]{3,2,1,0:T(8,128)S(1)}, f32[2,6,6,640]{3,2,1,0:T(8,128)}, u32[]{:S(2)}, u32[]{:S(2)}) collective-permute-start(f32[2,6,6,640]{3,2,1,0:T(8,128)S(1)} %get-tuple-element.32), channel_id=1, source_target_pairs={{4,1},{5,2},{6,3},{8,5},{9,6},{10,7},{12,9},{13,10},{14,11},{20,17... | collective-permute-start | bytes 552968 | tf_op jit(solution)/shard_map/ppermute | solution.py:39
  21.4 40.8 %collective-permute-start.4 = (f32[2,8,6,640]{3,2,1,0:T(8,128)S(1)}, f32[2,8,6,640]{3,2,1,0:T(8,128)S(1)}, u32[]{:S(2)}, u32[]{:S(2)}) collective-permute-start(f32[2,8,6,640]{3,2,1,0:T(8,128)S(1)} %get-tuple-element.37), channel_id=1, source_target_pairs={{1,0},{2,1},{3,2},{5,4},{6,5},{7,6},{9,8},{10,9},{11,10},{13,12},{... | collective-permute-start | bytes 737288 | tf_op jit(solution)/shard_map/ppermute | solution.py:39
  24.0 18.0 %collective-permute-start.2 = (f32[2,6,6,640]{3,2,1,0:T(8,128)S(1)}, f32[2,6,6,640]{3,2,1,0:T(8,128)}, u32[]{:S(2)}, u32[]{:S(2)}) collective-permute-start(f32[2,6,6,640]{3,2,1,0:T(8,128)S(1)} %get-tuple-element.31), channel_id=1, source_target_pairs={{1,4},{2,5},{3,6},{5,8},{6,9},{7,10},{9,12},{10,13},{11,14},{17,20... | collective-permute-start | bytes 552968 | tf_op jit(solution)/shard_map/ppermute | solution.py:39
  28.5 36.6 %all-to-all-start.1 = ((f32[4,16,2560]{2,0,1:T(4,128)}), f32[4,16,2560]{2,0,1:T(4,128)S(1)}, u32[]{:S(2)}, u32[]{:S(2)}) async-start(f32[4,16,2560]{2,0,1:T(4,128)} %broadcast_in_dim.97), calls=%async_computation.1 | async-start | bytes 1310720 | tf_op jit(solution)/shard_map/all_to_all | solution.py:169
  35.7 26.5 %copy-start.2 = (f32[2,6,6,640]{3,2,1,0:T(8,128)}, f32[2,6,6,640]{3,2,1,0:T(8,128)S(1)}, u32[]{:S(2)}) copy-start(f32[2,6,6,640]{3,2,1,0:T(8,128)S(1)} %collective-permute-done.7) | copy-start | bytes 552964
  35.8 26.5 %collective-permute-start.3 = (f32[2,8,6,640]{3,2,1,0:T(8,128)S(1)}, f32[2,8,6,640]{3,2,1,0:T(8,128)S(1)}, u32[]{:S(2)}, u32[]{:S(2)}) collective-permute-start(f32[2,8,6,640]{3,2,1,0:T(8,128)S(1)} %get-tuple-element.36), channel_id=1, source_target_pairs={{0,1},{1,2},{2,3},{4,5},{5,6},{6,7},{8,9},{9,10},{10,11},{12,13},{... | collective-permute-start | bytes 737288 | tf_op jit(solution)/shard_map/ppermute | solution.py:39
  40.0 23.0 %collective-permute-start.1 = (f32[2,6,8,640]{3,2,1,0:T(8,128)}, f32[2,6,8,640]{3,2,1,0:T(8,128)S(1)}, u32[]{:S(2)}, u32[]{:S(2)}) collective-permute-start(f32[2,6,8,640]{3,2,1,0:T(8,128)} %get-tuple-element.34), channel_id=1, source_target_pairs={{0,4},{1,5},{2,6},{3,7},{4,8},{5,9},{6,10},{7,11},{8,12},{9,13},{1... | collective-permute-start | bytes 737288 | tf_op jit(solution)/shard_map/ppermute | solution.py:39
  42.0 20.2 %collective-permute-start = (f32[2,6,6,640]{3,2,1,0:T(8,128)S(1)}, f32[2,6,6,640]{3,2,1,0:T(8,128)S(1)}, u32[]{:S(2)}, u32[]{:S(2)}) collective-permute-start(f32[2,6,6,640]{3,2,1,0:T(8,128)S(1)} %get-tuple-element.30), channel_id=1, source_target_pairs={{0,5},{1,6},{2,7},{4,9},{5,10},{6,11},{8,13},{9,14},{10,15},{16,21... | collective-permute-start | bytes 552968 | tf_op jit(solution)/shard_map/ppermute | solution.py:39
  62.2 0.7 copy-start.3
  62.2 0.8 copy-start.1
  82.5 21.2 %all-to-all-start.2 = ((f32[3,16,2560]{2,0,1:T(4,128)}), f32[3,16,2560]{2,0,1:T(4,128)S(1)}, u32[]{:S(2)}, u32[]{:S(2)}) async-start(f32[3,16,2560]{2,0,1:T(4,128)} %copy.11), calls=%async_computation.2 | async-start | bytes 1310720 | tf_op jit(solution)/shard_map/all_to_all | solution.py:184
  104.7 14.5 %all-to-all-start.3 = ((f32[3,16,2560]{2,0,1:T(4,128)}), f32[3,16,2560]{2,0,1:T(4,128)S(1)}, u32[]{:S(2)}, u32[]{:S(2)}) async-start(f32[3,16,2560]{2,0,1:T(4,128)} %broadcast_in_dim.103), calls=%async_computation.3 | async-start | bytes 1310720 | tf_op jit(solution)/shard_map/all_to_all | solution.py:186
